TPU v7x, 256 devices: a whole 4x4x8 slice. The times are simulated.
256 devices in a mesh: people: 2 (over x_hi), tm: 64 (over z, y, core), type: 2 (over x_lo).
Axes of the slice: x: 4 (x_hi: 2, x_lo: 2; x = x_hi * 2 + x_lo), y: 4, z: 8, core: 2. Of those that a mesh axis runs over, the one named last changes fastest.
Arguments:
- features: bfloat16 [3, 2, 16384], P(None, 'people', 'tm'), may hold values from -6 to 6
- wear: int32 [2, 16384], P('people', 'tm'), may hold values 0 or 1
- rec_start: int32 [2], P('people'), may hold values from 0 to 255
- rec_end: int32 [2], P('people'), may hold values from 16129 to 16384
- conv_first: bfloat16 [3, 3, 128], replicated, may hold values from -2 to 2
- conv_second: bfloat16 [3, 128, 128], replicated, may hold values from -0.3125 to 0.3125
- emit_weight: bfloat16 [128, 512], P(None, 'type'), may hold values from -0.5 to 0.5
- leave: float32 [8, 64], P('type'), may hold values from 0.002 to 0.5
- jump: float32 [8, 64, 64], P('type'), may hold values from -6 to 6
- init_logits: float32 [8, 64], P('type'), may hold values from -6 to 6
- type_prior: float32 [8], replicated, may hold values from -4 to 4
Outputs:
- loglik_rate: float32 [2, 8], P('people', 'type')
- type_post: float32 [2, 8], P('people', 'type')
- occupancy: float32 [8, 64], P('type')
- filtered: float32 [2, 16384, 8, 64], P('people', 'tm', 'type')
All inputs are finite; a program needn't handle non-finite values. No bound on the sum of `wear` on one device may be relied on, other than what follows from the above.
Results may differ from a plain program's by a relative error of at most 0.0085.
Values may be sent and summed in bfloat16 or wider, within the bound.
No kernel may reach another device: no remote copies, remote signals or barrier semaphores. Data moves between devices by JAX's collectives and lax.ppermute only.
A program may use at most 64 MiB of HBM per device.

v0:
```python
import jax
import jax.numpy as jnp
from jax import lax
from jax.sharding import PartitionSpec as P

HIGHEST = lax.Precision.HIGHEST
HIGH = lax.Precision.HIGH
TM_SPLIT = (8, 4, 2)
TM = ("tz", "ty", "tc")


def padded(block, sides, width):
    for axis, dim in sides:
        count = 1
        for name in axis:
            count *= lax.axis_size(name)
        forward = [(i, i + 1) for i in range(count - 1)]
        backward = [(target, source) for source, target in forward]
        low = lax.ppermute(
            lax.slice_in_dim(block, block.shape[dim] - width, None, axis=dim), axis, forward
        )
        high = lax.ppermute(lax.slice_in_dim(block, 0, width, axis=dim), axis, backward)
        block = jnp.concatenate([low, block, high], axis=dim)
    return block


def norm_mat(m):
    return m / jnp.sum(m, axis=(-2, -1), keepdims=True)


def norm_vec(v):
    return v / jnp.sum(v, axis=-1, keepdims=True)


def mat_mat(a, b):
    return jnp.einsum("...im,...ml->...il", a, b, precision=HIGH)


def bit_reverse(x, axis):
    bits = x.shape[axis].bit_length() - 1
    split = x.shape[:axis] + (2,) * bits + x.shape[axis + 1 :]
    perm = (
        list(range(axis))
        + [axis + bits - 1 - i for i in range(bits)]
        + list(range(axis + bits, len(split)))
    )
    return jnp.transpose(x.reshape(split), perm).reshape(x.shape)


def chain(mats):
    while len(mats) > 1:
        half = len(mats) // 2
        left = jnp.stack(mats[0 : 2 * half : 2])
        right = jnp.stack(mats[1 : 2 * half : 2])
        joined = norm_mat(mat_mat(left, right))
        mats = [joined[i] for i in range(half)] + mats[2 * half :]
    return mats[0]


def group_scan(mats, axis, whole=True):
    count = lax.axis_size(axis)
    mine = lax.axis_index(axis)
    eye = jnp.eye(mats.shape[-1], dtype=mats.dtype)
    everyone = lax.all_gather(mats, axis)
    earlier = [jnp.where(mine > j, everyone[j], eye) for j in range(count)]
    if not whole:
        return chain(earlier), None
    both = chain([jnp.stack([earlier[j], everyone[j]]) for j in range(count)])
    return both[0], both[1]


def exclusive_scan(mats, axes):
    parts = []
    for depth, axis in enumerate(reversed(axes)):
        before, mats = group_scan(mats, axis, depth < len(axes) - 1)
        parts.append(before)
    return chain(parts[::-1])


def on_device(
    features,
    wear,
    rec_start,
    rec_end,
    conv_first,
    conv_second,
    emit_weight,
    leave,
    jump,
    init_logits,
    type_prior,
):
    persons = features.shape[1]
    span = features.shape[2]
    kinds = jump.shape[0]
    states = jump.shape[-1]
    tm_index = lax.axis_index(TM)
    type_index = lax.axis_index("type")
    people_index = lax.axis_index("people")
    tm_count = 1
    for axis in TM:
        tm_count *= lax.axis_size(axis)
    total_epochs = span * tm_count
    extended = padded(features, ((TM, 2),), 5)
    first = jnp.zeros((persons, span + 8, conv_first.shape[2]), jnp.float32)
    for tap in range(3):
        first = first + jnp.einsum(
            "ipt,ic->ptc",
            extended[:, :, tap : tap + span + 8],
            conv_first[tap],
            preferred_element_type=jnp.float32,
        )
    wide_pos = tm_index * span - 4 + jnp.arange(span + 8, dtype=jnp.int32)
    inside = (wide_pos >= 0) & (wide_pos < total_epochs)
    first = jnp.where(inside[None, :, None], jax.nn.silu(first), 0.0).astype(jnp.bfloat16)
    second = jnp.zeros((persons, span, conv_second.shape[2]), jnp.float32)
    for tap in range(3):
        second = second + jnp.einsum(
            "ptc,cd->ptd",
            first[:, 4 * tap : 4 * tap + span],
            conv_second[tap],
            preferred_element_type=jnp.float32,
        )
    second = jax.nn.silu(second).astype(jnp.bfloat16)
    logits = jnp.einsum("ptc,cm->ptm", second, emit_weight, preferred_element_type=jnp.float32)
    probs = jnp.exp(jax.nn.log_softmax(logits.reshape(persons, span, kinds, states), axis=-1))
    positions = tm_index * span + jnp.arange(span, dtype=jnp.int32)
    observed = (
        (wear > 0)
        & (positions[None, :] >= rec_start[:, None])
        & (positions[None, :] < rec_end[:, None])
    )
    emis = jnp.where(observed[:, :, None, None], probs, jnp.float32(1.0))
    observed_f = observed.astype(jnp.float32)
    eye_small = jnp.eye(states, dtype=jnp.float32)
    trans = (1.0 - leave)[..., None] * eye_small + leave[..., None] * jax.nn.softmax(jump, axis=-1)
    start = jax.nn.softmax(init_logits, axis=-1)

    order = bit_reverse(jnp.transpose(emis, (2, 0, 1, 3)), 2)
    half = span // 2
    e_even = order[:, :, :half]
    e_odd = order[:, :, half:]
    quarter = span // 4
    cols = [order[:, :, m * quarter : (m + 1) * quarter, None, :] for m in range(4)]
    left = trans[:, None, None] * cols[0]
    pair = norm_mat(jnp.einsum("kpjim,kml->kpjil", left, trans, precision=HIGH) * cols[2])
    level = norm_mat(jnp.einsum("kpjim,kml->kpjil", pair, trans, precision=HIGH) * cols[1])
    level = norm_mat(jnp.einsum("kpjim,kml->kpjil", level, trans, precision=HIGH) * cols[3])
    levels = [None, pair, level]
    while levels[-1].shape[2] > 1:
        last = levels[-1]
        n = last.shape[2] // 2
        levels.append(norm_mat(mat_mat(last[:, :, :n], last[:, :, n:])))
    device_op = levels[-1][:, :, 0]

    before = exclusive_scan(device_op, TM)
    alpha_in = norm_vec(jnp.einsum("ki,kpij->kpj", start, before, precision=HIGHEST))

    entry = alpha_in[:, :, None]
    for depth in range(len(levels) - 1, 1, -1):
        n = entry.shape[2]
        sibling = levels[depth - 1][:, :, :n]
        moved = norm_vec(jnp.einsum("kpni,kpnil->kpnl", entry, sibling, precision=HIGH))
        entry = jnp.concatenate([entry, moved], axis=2)
    u = jnp.einsum("kpji,kil->kpjl", entry, trans, precision=HIGH) * e_even
    c_even = jnp.sum(u, axis=-1)
    a_even = u / c_even[..., None]
    v = jnp.einsum("kpji,kil->kpjl", a_even, trans, precision=HIGH) * e_odd
    c_odd = jnp.sum(v, axis=-1)
    a_odd = v / c_odd[..., None]
    alpha = bit_reverse(jnp.concatenate([a_even, a_odd], axis=2), 2)
    filtered = jnp.transpose(alpha, (1, 2, 0, 3))
    own_log = jnp.transpose(jnp.sum(jnp.log(c_even), axis=2) + jnp.sum(jnp.log(c_odd), axis=2))
    occupied = jnp.einsum("pt,ptks->pks", observed_f, filtered, precision=HIGHEST)
    count = jnp.sum(observed_f, axis=1)

    halves_n = lax.axis_size("type")
    people_n = lax.axis_size("people") * persons
    row = jnp.concatenate(
        [own_log, occupied.reshape(persons, kinds * states), count[:, None]], axis=1
    )
    person_hot = (
        people_index * persons + jnp.arange(persons)[:, None] == jnp.arange(people_n)[None, :]
    ).astype(jnp.float32)
    half_hot = (type_index == jnp.arange(halves_n)).astype(jnp.float32)
    table = person_hot[:, :, None, None] * half_hot[None, None, :, None] * row[:, None, None, :]
    table = jnp.sum(table, axis=0)
    for axis in TM[::-1] + (("people", "type"),):
        table = lax.psum(table, axis)

    full = table[:, :, :kinds].reshape(people_n, halves_n * kinds)
    rate_full = full / total_epochs
    post_full = jax.nn.softmax(type_prior[None, :] + 8.0 * rate_full, axis=-1)
    offset = type_index * kinds
    mine = people_index * persons
    rate_own = lax.dynamic_slice(rate_full, (mine, offset), (persons, kinds))
    post_own = lax.dynamic_slice(post_full, (mine, offset), (persons, kinds))
    post_type = lax.dynamic_slice(post_full, (jnp.int32(0), offset), (people_n, kinds))
    occ_all = jnp.take(table, type_index, axis=1)[:, kinds : kinds + kinds * states]
    occ_all = occ_all.reshape(people_n, kinds, states)
    cnt_all = jnp.take(table, type_index, axis=1)[:, kinds + kinds * states]
    numer = jnp.einsum("pk,pks->ks", post_type, occ_all, precision=HIGHEST)
    denom = jnp.einsum("pk,p->k", post_type, cnt_all, precision=HIGHEST)
    occupancy = numer / denom[:, None]
    return (rate_own, post_own, occupancy, filtered)


def solution(mesh):
    people, epochs, halves = mesh.devices.shape
    assert epochs == TM_SPLIT[0] * TM_SPLIT[1] * TM_SPLIT[2]
    fine = jax.sharding.Mesh(
        mesh.devices.reshape((people,) + TM_SPLIT + (halves,)), ("people",) + TM + ("type",)
    )
    return jax.shard_map(
        on_device,
        mesh=fine,
        in_specs=(
            P(None, "people", TM),
            P("people", TM),
            P("people"),
            P("people"),
            P(),
            P(),
            P(None, "type"),
            P("type", None),
            P("type", None, None),
            P("type", None),
            P(),
        ),
        out_specs=(
            P("people", "type"),
            P("people", "type"),
            P("type", None),
            P("people", TM, "type", None),
        ),
        check_vma=False,
    )
```

profile of v0, /device:TPU:4, one launch (start us, length us, event | category | flops | bytes accessed | tf_op | source)
XLA Modules:
  0.0 205.2 jit_solution(7661266490407921474)
XLA Ops:
  1.4 1.3 collective-permute-start.1
  2.7 3.0 %collective-permute-start = (bf16[3,1,5]{2,0,1:T(4,128)(2,1)S(1)}, bf16[3,1,5]{2,0,1:T(4,128)(2,1)S(1)}, u32[]{:S(2)}, u32[]{:S(2)}) collective-permute-start(bf16[3,1,5]{2,0,1:T(4,128)(2,1)S(1)} %get-tuple-element.63), channel_id=1, source_target_pairs={{0,2},{2,4},{4,6},{6,8},{8,10},{10,12},{12,14},{14,16},{16,18},{18... | collective-permute-start | bytes 98 | tf_op jit(solution)/shard_map/ppermute | solution.py:19
  9.2 1.2 fusion.135
  19.9 1.1 bitcast_reduce_fusion
  23.4 4.6 %multiply_reduce_fusion.3 = (f32[4,64]{1,0:T(4,128)S(1)}, f32[4,64,64,64]{3,2,1,0:T(8,128)S(1)}) fusion(f32[4,64,64]{2,1,0:T(8,128)S(1)} %get-tuple-element.52, f32[4,64,64]{2,1,0:T(8,128)S(1)} %multiply_add_fusion, f32[4,64,64]{2,1,0:T(8,128)S(1)} %get-tuple-element.53), kind=kOutput, calls=%fused_computation.15 | convolution fusion | flops 405798656 | bytes 4391936 | tf_op jit(solution)/shard_map/kpjim,kml->kpjil/dot_general | solution.py:146
  27.9 5.1 %multiply_reduce_fusion.2 = (f32[4,64]{1,0:T(4,128)S(1)}, f32[4,64,64,64]{3,2,1,0:T(8,128)S(1)}) fusion(f32[4,64,64]{2,1,0:T(8,128)S(1)} %get-tuple-element.51, f32[4,64,64]{2,1,0:T(8,128)S(1)} %multiply_add_fusion, f32[4,64,64,64]{3,2,1,0:T(8,128)S(1)} %get-tuple-element.70, f32[4,64]{1,0:T(4,128)S(1)} %get-tuple-element.69, ...), kind=kOutput, calls=%fused_computation.13 | convolution fusion | flops 406847232 | bytes 8587264 | tf_op jit(solution)/shard_map/kpjim,kml->kpjil/dot_general | solution.py:147
  33.0 5.3 %multiply_reduce_fusion.1 = (f32[4,64]{1,0:T(4,128)S(1)}, f32[4,64,64,64]{3,2,1,0:T(8,128)S(1)}) fusion(f32[4,64,64]{2,1,0:T(8,128)S(1)} %get-tuple-element.50, f32[4,64,64]{2,1,0:T(8,128)S(1)} %multiply_add_fusion, f32[4,64,64,64]{3,2,1,0:T(8,128)S(1)} %get-tuple-element.72, f32[4,64]{1,0:T(4,128)S(1)} %get-tuple-element.71, ...), kind=kOutput, calls=%fused_computation.11 | convolution fusion | flops 406847232 | bytes 8587264 | tf_op jit(solution)/shard_map/kpjim,kml->kpjil/dot_general | solution.py:148
  38.3 1.7 divide_bitcast_fusion
  40.0 3.1 %fusion.136 = (f32[4,32]{1,0:T(4,128)S(1)}, f32[4,32,64,64]{3,2,1,0:T(8,128)S(1)}) fusion(f32[4,1,64,64,64]{4,3,2,0,1:T(8,128)S(1)} %divide_bitcast_fusion), kind=kOutput, calls=%fused_computation.266 | convolution fusion | flops 201850752 | bytes 6291968 | tf_op jit(solution)/shard_map/...im,...ml->...il/dot_general | solution.py:36
  43.6 1.4 fusion.137
  48.0 2.8 %all-gather = f32[8,64,64]{2,1,0:T(8,128)S(1)} all-gather(f32[4,64,64]{2,1,0:T(8,128)S(1)} %broadcast_divide_fusion.5), channel_id=2, replica_groups=mesh['people'=2,'tz'=8,'ty'=4,'tc'=2,'type'=2] {'tc'}, dimensions={0}, use_global_device_ids=true | all-gather | bytes 196608 | tf_op jit(solution)/shard_map/all_gather | solution.py:64
  51.4 15.2 %all-gather.1 = f32[4,1,4,1,64,64]{5,4,3,2,1,0:T(8,128)S(1)} all-gather(f32[1,1,4,1,64,64]{5,4,3,2,1,0:T(8,128)S(1)} %slice_bitcast_fusion.53), channel_id=3, replica_groups=mesh['people'=2,'tz'=8,'ty'=4,'tc'=2,'type'=2] {'ty'}, dimensions={0}, use_global_device_ids=true | all-gather | bytes 327680 | tf_op jit(solution)/shard_map/all_gather | solution.py:64
  67.9 30.5 %all-gather.2 = f32[8,1,4,1,64,64]{5,4,3,2,1,0:T(8,128)S(1)} all-gather(f32[1,1,4,1,64,64]{5,4,3,2,1,0:T(8,128)S(1)} %slice_bitcast_fusion.48), channel_id=4, replica_groups=mesh['people'=2,'tz'=8,'ty'=4,'tc'=2,'type'=2] {'tz'}, dimensions={0}, use_global_device_ids=true | all-gather | bytes 589824 | tf_op jit(solution)/shard_map/all_gather | solution.py:64
  101.4 1.1 fusion.92
  103.6 1.2 fusion.64
  105.5 1.6 fusion.26
  109.7 2.5 %fusion.17 = f32[4,16,1,64]{3,2,1,0:T(1,128)S(1)} fusion(f32[4,16,64,1]{2,3,1,0:T(1,128)S(1)} %bitcast.462, f32[4,1,32,64,64]{4,3,2,0,1:T(8,128)} %copy-done.4), kind=kOutput, calls=%fused_computation.30 | convolution fusion | flops 1572864 | bytes 2129920 | tf_op jit(solution)/shard_map/kpni,kpnil->kpnl/dot_general | solution.py:163
  112.5 1.3 concatenate.41
  113.8 2.9 %multiply_reduce_fusion.4 = f32[4,32,64]{2,1,0:T(8,128)S(1)} fusion(f32[4,1,64,64,64]{4,3,2,0,1:T(8,128)} %copy-done.2, f32[4,32,64]{2,1,0:T(8,128)S(1)} %copy.156), kind=kLoop, calls=%fused_computation.19 | loop fusion | flops 1040384 | bytes 2162688
  117.4 5.9 %multiply_reduce_fusion = f32[4,64,64]{2,1,0:T(8,128)S(1)} fusion(f32[4,64,64]{2,1,0:T(8,128)S(1)} %copy.157, f32[4,64]{1,0:T(4,128)S(1)} %get-tuple-element.69, f32[4,64,64,64]{3,2,1,0:T(8,128)} %copy-done.3, f32[4,64,64]{2,1,0:T(8,128)} %copy-done.9), kind=kLoop, calls=%fused_computation.5 | loop fusion | flops 4177920 | bytes 4391936
  127.0 3.9 %psum.28 = f32[2,2,261]{0,2,1:T(8,128)S(1)} all-reduce(f32[2,2,261]{0,2,1:T(8,128)S(1)} %broadcast_multiply_fusion), channel_id=1, replica_groups=mesh['people'=2,'tz'=8,'ty'=4,'tc'=2,'type'=2] {'tc'}, use_global_device_ids=true, to_apply=%region_36.37 | all-reduce | flops 1044 | bytes 8352 | tf_op jit(solution)/shard_map/psum | solution.py:189
  130.9 20.8 %psum.29 = f32[2,2,261]{0,2,1:T(8,128)S(1)} all-reduce(f32[2,2,261]{0,2,1:T(8,128)S(1)} %psum.28), channel_id=1, replica_groups=mesh['people'=2,'tz'=8,'ty'=4,'tc'=2,'type'=2] {'ty'}, use_global_device_ids=true, to_apply=%region_37.38 | all-reduce | flops 1044 | bytes 8352 | tf_op jit(solution)/shard_map/psum | solution.py:189
  151.8 31.5 %psum.30 = f32[2,2,261]{0,2,1:T(8,128)S(1)} all-reduce(f32[2,2,261]{0,2,1:T(8,128)S(1)} %psum.29), channel_id=1, replica_groups=mesh['people'=2,'tz'=8,'ty'=4,'tc'=2,'type'=2] {'tz'}, use_global_device_ids=true, to_apply=%region_38.39 | all-reduce | flops 1044 | bytes 8352 | tf_op jit(solution)/shard_map/psum | solution.py:189
  183.2 18.1 %psum.31 = f32[2,2,261]{0,2,1:T(8,128)S(1)} all-reduce(f32[2,2,261]{0,2,1:T(8,128)S(1)} %psum.30), channel_id=1, replica_groups=mesh['people'=2,'tz'=8,'ty'=4,'tc'=2,'type'=2] {'people','type'}, use_global_device_ids=true, to_apply=%region_39.40 | all-reduce | flops 1044 | bytes 8352 | tf_op jit(solution)/shard_map/psum | solution.py:189
  (153 shorter events, 35.5 us)
Async XLA Ops:
  0.6 19.3 %copy-start = (bf16[128,256]{1,0:T(8,128)(2,1)S(1)}, bf16[128,256]{1,0:T(8,128)(2,1)}, u32[]{:S(2)}) copy-start(bf16[128,256]{1,0:T(8,128)(2,1)} %param.19) | copy-start | bytes 196612
  1.4 13.0 %collective-permute-start.1 = (bf16[3,1,5]{2,0,1:T(4,128)(2,1)S(1)}, bf16[3,1,5]{2,0,1:T(4,128)(2,1)S(1)}, u32[]{:S(2)}, u32[]{:S(2)}) collective-permute-start(bf16[3,1,5]{2,0,1:T(4,128)(2,1)S(1)} %get-tuple-element.64), channel_id=1, source_target_pairs={{2,0},{4,2},{6,4},{8,6},{10,8},{12,10},{14,12},{16,14},{18,16},{20... | collective-permute-start | bytes 98 | tf_op jit(solution)/shard_map/ppermute | solution.py:22
  2.7 11.7 %collective-permute-start = (bf16[3,1,5]{2,0,1:T(4,128)(2,1)S(1)}, bf16[3,1,5]{2,0,1:T(4,128)(2,1)S(1)}, u32[]{:S(2)}, u32[]{:S(2)}) collective-permute-start(bf16[3,1,5]{2,0,1:T(4,128)(2,1)S(1)} %get-tuple-element.63), channel_id=1, source_target_pairs={{0,2},{2,4},{4,6},{6,8},{8,10},{10,12},{12,14},{14,16},{16,18},{18... | collective-permute-start | bytes 98 | tf_op jit(solution)/shard_map/ppermute | solution.py:19
  23.4 9.6 %copy-start.9 = (f32[4,64,64]{2,1,0:T(8,128)}, f32[4,64,64]{2,1,0:T(8,128)S(1)}, u32[]{:S(2)}) copy-start(f32[4,64,64]{2,1,0:T(8,128)S(1)} %get-tuple-element.52) | copy-start | bytes 196612
  27.9 5.1 %copy-start.3 = (f32[4,64,64,64]{3,2,1,0:T(8,128)}, f32[4,64,64,64]{3,2,1,0:T(8,128)S(1)}, u32[]{:S(2)}) copy-start(f32[4,64,64,64]{3,2,1,0:T(8,128)S(1)} %get-tuple-element.70) | copy-start | bytes 12582916
  40.0 3.6 %copy-start.2 = (f32[4,1,64,64,64]{4,3,2,0,1:T(8,128)}, f32[4,1,64,64,64]{4,3,2,0,1:T(8,128)S(1)}, u32[]{:S(2)}) copy-start(f32[4,1,64,64,64]{4,3,2,0,1:T(8,128)S(1)} %divide_bitcast_fusion) | copy-start | bytes 12582916
  43.6 3.0 %copy-start.4 = (f32[4,1,32,64,64]{4,3,2,0,1:T(8,128)}, f32[4,1,32,64,64]{4,3,2,0,1:T(8,128)S(1)}, u32[]{:S(2)}) copy-start(f32[4,1,32,64,64]{4,3,2,0,1:T(8,128)S(1)} %divide_bitcast_fusion.1) | copy-start | bytes 6291460
  46.7 4.6 %copy-start.5 = (f32[4,1,4,64,64]{4,3,2,0,1:T(8,128)}, f32[4,1,4,64,64]{4,3,2,0,1:T(8,128)S(1)}, u32[]{:S(2)}) copy-start(f32[4,1,4,64,64]{4,3,2,0,1:T(8,128)S(1)} %divide_bitcast_fusion.4) | copy-start | bytes 786436
  47.2 0.7 copy-start.8
  108.4 8.6 %copy-start.6 = (f32[4,1,1,64]{2,3,0,1:T(8,128)S(1)}, f32[4,1,1,64]{2,3,0,1:T(8,128)}, u32[]{:S(2)}) copy-start(f32[4,1,1,64]{2,3,0,1:T(8,128)} %copy.111) | copy-start | bytes 3076
  108.4 8.6 %copy-start.7 = (f32[4,1,2,64]{2,3,0,1:T(8,128)S(1)}, f32[4,1,2,64]{2,3,0,1:T(8,128)}, u32[]{:S(2)}) copy-start(f32[4,1,2,64]{2,3,0,1:T(8,128)} %fusion.26) | copy-start | bytes 6148
  112.3 11.2 %copy-start.11 = (f32[4,1,128,64]{3,2,0,1:T(8,128)S(1)}, f32[4,1,128,64]{3,2,0,1:T(8,128)}, u32[]{:S(2)}) copy-start(f32[4,1,128,64]{3,2,0,1:T(8,128)} %get-tuple-element.55) | copy-start | bytes 393220
  112.5 11.2 %copy-start.10 = (f32[4,1,128,64]{3,2,0,1:T(8,128)S(1)}, f32[4,1,128,64]{3,2,0,1:T(8,128)}, u32[]{:S(2)}) copy-start(f32[4,1,128,64]{3,2,0,1:T(8,128)} %get-tuple-element.54) | copy-start | bytes 393220
  117.3 87.9 %copy-start.1 = (bf16[128,256]{1,0:T(8,128)(2,1)S(1)}, bf16[128,256]{1,0:T(8,128)(2,1)}, u32[]{:S(2)}) copy-start(bf16[128,256]{1,0:T(8,128)(2,1)} %param.19) | copy-start | bytes 196612
  117.4 84.2 %copy-start.12 = (f32[8]{0:T(128)S(1)}, f32[8]{0:T(128)}, u32[]{:S(2)}) copy-start(f32[8]{0:T(128)} %param.23) | copy-start | bytes 100
where the time goes:
time: 206 us; the launch traced here: 205 us
  blocking collectives  123 us (60%)
  matrix products  37.4 us (18%)
  other arithmetic  25.4 us (12%)
  local copies, waits for them, and re-layouts  12.5 us (6%)
  starting transfers between devices  4.31 us (2%)
  between operations  2.76 us (1%)
    psum x4, blocking collectives, on_device(): table = lax.psum(table, axis)  74.2 us
    all_gather x3, blocking collectives, group_scan(): everyone = lax.all_gather(mats, axis)  48.6 us
    dot_general x14, matrix products, mat_mat(): return jnp.einsum('...im,...ml->...il', a, b, precision=HIGH)  9.46 us
    unnamed x2, other arithmetic  8.83 us
    dot_general x5, matrix products, on_device(): jnp.einsum('kpni,kpnil->kpnl', entry, sibling, precision=HIGH)  5.62 us
    dot_general x1, matrix products, on_device(): jnp.einsum('kpjim,kml->kpjil', level, trans, precision=HIGH) * cols[3]  5.28 us
    dot_general x1, matrix products, on_device(): jnp.einsum('kpjim,kml->kpjil', pair, trans, precision=HIGH) * cols[1]  5.06 us
    dot_general x1, matrix products, on_device(): jnp.einsum('kpjim,kml->kpjil', left, trans, precision=HIGH) * cols[2]  4.56 us
  transfers between devices with their start and end apart: 2, of which 0 were waited for; matrix products, arithmetic and copies ran while one was open for 4% of the time, Pallas kernels for 0%

commit v1 on v0

--- a/solution.py
+++ b/solution.py
@@ -48,12 +48,11 @@
 
 
 def chain(mats):
-    while len(mats) > 1:
-        half = len(mats) // 2
-        left = jnp.stack(mats[0 : 2 * half : 2])
-        right = jnp.stack(mats[1 : 2 * half : 2])
-        joined = norm_mat(mat_mat(left, right))
-        mats = [joined[i] for i in range(half)] + mats[2 * half :]
+    while mats.shape[0] > 1:
+        half = mats.shape[0] // 2
+        paired = mats[: 2 * half].reshape((half, 2) + mats.shape[1:])
+        joined = norm_mat(mat_mat(paired[:, 0], paired[:, 1]))
+        mats = jnp.concatenate([joined, mats[2 * half :]], axis=0)
     return mats[0]
 
 
@@ -62,10 +61,11 @@
     mine = lax.axis_index(axis)
     eye = jnp.eye(mats.shape[-1], dtype=mats.dtype)
     everyone = lax.all_gather(mats, axis)
-    earlier = [jnp.where(mine > j, everyone[j], eye) for j in range(count)]
+    keep = (jnp.arange(count) < mine).reshape((count,) + (1,) * mats.ndim)
+    earlier = jnp.where(keep, everyone, eye)
     if not whole:
         return chain(earlier), None
-    both = chain([jnp.stack([earlier[j], everyone[j]]) for j in range(count)])
+    both = chain(jnp.stack([earlier, everyone], axis=1))
     return both[0], both[1]
 
 
@@ -74,7 +74,7 @@
     for depth, axis in enumerate(reversed(axes)):
         before, mats = group_scan(mats, axis, depth < len(axes) - 1)
         parts.append(before)
-    return chain(parts[::-1])
+    return chain(jnp.stack(parts[::-1]))
 
 
 def on_device(
@@ -102,25 +102,17 @@
         tm_count *= lax.axis_size(axis)
     total_epochs = span * tm_count
     extended = padded(features, ((TM, 2),), 5)
-    first = jnp.zeros((persons, span + 8, conv_first.shape[2]), jnp.float32)
-    for tap in range(3):
-        first = first + jnp.einsum(
-            "ipt,ic->ptc",
-            extended[:, :, tap : tap + span + 8],
-            conv_first[tap],
-            preferred_element_type=jnp.float32,
-        )
+    taps_first = jnp.stack([extended[:, :, tap : tap + span + 8] for tap in range(3)])
+    first = jnp.einsum(
+        "jipt,jic->ptc", taps_first, conv_first, preferred_element_type=jnp.float32
+    )
     wide_pos = tm_index * span - 4 + jnp.arange(span + 8, dtype=jnp.int32)
     inside = (wide_pos >= 0) & (wide_pos < total_epochs)
     first = jnp.where(inside[None, :, None], jax.nn.silu(first), 0.0).astype(jnp.bfloat16)
-    second = jnp.zeros((persons, span, conv_second.shape[2]), jnp.float32)
-    for tap in range(3):
-        second = second + jnp.einsum(
-            "ptc,cd->ptd",
-            first[:, 4 * tap : 4 * tap + span],
-            conv_second[tap],
-            preferred_element_type=jnp.float32,
-        )
+    taps_second = jnp.stack([first[:, 4 * tap : 4 * tap + span] for tap in range(3)])
+    second = jnp.einsum(
+        "jptc,jcd->ptd", taps_second, conv_second, preferred_element_type=jnp.float32
+    )
     second = jax.nn.silu(second).astype(jnp.bfloat16)
     logits = jnp.einsum("ptc,cm->ptm", second, emit_weight, preferred_element_type=jnp.float32)
     probs = jnp.exp(jax.nn.log_softmax(logits.reshape(persons, span, kinds, states), axis=-1))
@@ -144,8 +136,11 @@
     cols = [order[:, :, m * quarter : (m + 1) * quarter, None, :] for m in range(4)]
     left = trans[:, None, None] * cols[0]
     pair = norm_mat(jnp.einsum("kpjim,kml->kpjil", left, trans, precision=HIGH) * cols[2])
-    level = norm_mat(jnp.einsum("kpjim,kml->kpjil", pair, trans, precision=HIGH) * cols[1])
-    level = norm_mat(jnp.einsum("kpjim,kml->kpjil", level, trans, precision=HIGH) * cols[3])
+    def extend(carry, col):
+        grown = jnp.einsum("kpjim,kml->kpjil", carry, trans, precision=HIGH) * col
+        return norm_mat(grown), None
+
+    level, _ = lax.scan(extend, pair, jnp.stack([cols[1], cols[3]]))
     levels = [None, pair, level]
     while levels[-1].shape[2] > 1:
         last = levels[-1]
@@ -154,7 +149,7 @@
     device_op = levels[-1][:, :, 0]
 
     before = exclusive_scan(device_op, TM)
-    alpha_in = norm_vec(jnp.einsum("ki,kpij->kpj", start, before, precision=HIGHEST))
+    alpha_in = norm_vec(jnp.einsum("ki,kpij->kpj", start, before, precision=HIGH))
 
     entry = alpha_in[:, :, None]
     for depth in range(len(levels) - 1, 1, -1):
@@ -171,7 +166,7 @@
     alpha = bit_reverse(jnp.concatenate([a_even, a_odd], axis=2), 2)
     filtered = jnp.transpose(alpha, (1, 2, 0, 3))
     own_log = jnp.transpose(jnp.sum(jnp.log(c_even), axis=2) + jnp.sum(jnp.log(c_odd), axis=2))
-    occupied = jnp.einsum("pt,ptks->pks", observed_f, filtered, precision=HIGHEST)
+    occupied = jnp.einsum("pt,ptks->pks", observed_f, filtered, precision=HIGH)
     count = jnp.sum(observed_f, axis=1)
 
     halves_n = lax.axis_size("type")

time: 206 us -> 225 us (1.092)
  other arithmetic: 25.4 us -> 38.9 us
  matrix products: 37.4 us -> 41.6 us
    div x12 -> x14, other arithmetic: 3.33 us -> 14.2 us  [norm_mat(): return m / jnp.sum(m, axis=(-2, -1), keepdims=True)]
    dot_general x14, matrix products: 9.46 us -> 12.6 us  [mat_mat(): return jnp.einsum('...im,...ml->...il', a, b, precision=HIGH)]
    dot_general x9 -> x5, matrix products: 15.5 us -> 16.8 us  [the longest x2 15.4 us: extend(): grown = jnp.einsum('kpjim,kml->kpjil', carry, trans, precision=HIGH) * col]
where the time goes in v1:
time: 225 us; the launch traced here: 224 us
  blocking collectives  123 us (55%)
  matrix products  41.6 us (18%)
  other arithmetic  38.9 us (17%)
  local copies, waits for them, and re-layouts  13.9 us (6%)
  starting transfers between devices  4.31 us (2%)
  between operations  2.73 us (1%)
    psum x4, blocking collectives, on_device(): table = lax.psum(table, axis)  74.2 us
    all_gather x3, blocking collectives, group_scan(): everyone = lax.all_gather(mats, axis)  48.6 us
    dot_general x2, matrix products, extend(): grown = jnp.einsum('kpjim,kml->kpjil', carry, trans, precision=HIGH) * col  15.4 us
    div x14, other arithmetic, norm_mat(): return m / jnp.sum(m, axis=(-2, -1), keepdims=True)  14.2 us
    dot_general x14, matrix products, mat_mat(): return jnp.einsum('...im,...ml->...il', a, b, precision=HIGH)  12.6 us
    unnamed x2, other arithmetic  8.81 us
    dot_general x5, matrix products, on_device(): jnp.einsum('kpni,kpnil->kpnl', entry, sibling, precision=HIGH)  5.61 us
  transfers between devices with their start and end apart: 2, of which 0 were waited for; matrix products, arithmetic and copies ran while one was open for 4% of the time, Pallas kernels for 0%

profile of v1, /device:TPU:4, one launch (start us, length us, event | category | flops | bytes accessed | tf_op | source)
XLA Modules:
  0.0 224.4 jit_solution(3449130090498195968)
XLA Ops:
  1.5 1.3 collective-permute-start.1
  2.7 3.0 %collective-permute-start = (bf16[3,1,5]{2,0,1:T(4,128)(2,1)S(1)}, bf16[3,1,5]{2,0,1:T(4,128)(2,1)S(1)}, u32[]{:S(2)}, u32[]{:S(2)}) collective-permute-start(bf16[3,1,5]{2,0,1:T(4,128)(2,1)S(1)} %get-tuple-element.96), channel_id=1, source_target_pairs={{0,2},{2,4},{4,6},{6,8},{8,10},{10,12},{12,14},{14,16},{16,18},{18... | collective-permute-start | bytes 98 | tf_op jit(solution)/shard_map/ppermute | solution.py:19
  14.3 1.3 fusion.79
  22.0 4.3 %multiply_reduce_fusion.2 = (f32[4,64]{1,0:T(4,128)S(1)}, f32[4,64,64,64]{3,2,1,0:T(8,128)S(1)}) fusion(f32[4,64,64]{2,1,0:T(8,128)S(1)} %get-tuple-element.79, f32[4,64,64]{2,1,0:T(8,128)S(1)} %multiply_add_fusion, f32[4,64,64]{2,1,0:T(8,128)S(1)} %get-tuple-element.80), kind=kOutput, calls=%fused_computation.15 | convolution fusion | flops 405798656 | bytes 4391936 | tf_op jit(solution)/shard_map/kpjim,kml->kpjil/dot_general | solution.py:138
  26.3 4.6 %fusion.18 = f32[4,1,64,64,64]{4,3,2,0,1:T(8,128)} fusion(f32[4,64]{1,0:T(4,128)S(1)} %get-tuple-element.102, f32[4,64,64,64]{3,2,1,0:T(8,128)S(1)} %get-tuple-element.103, f32[4,64,64]{2,1,0:T(8,128)S(1)} %get-tuple-element.79), kind=kLoop, calls=%fused_computation.26 | loop fusion | flops 2097152 | bytes 8455168 | tf_op jit(solution)/shard_map/div | solution.py:28
  32.1 23.4 %while.11 = (s32[]{:T(128)}, f32[4,1,64,64,64]{4,3,2,0,1:T(8,128)}, f32[4,64,64]{2,1,0:T(8,128)S(1)}, f32[2,4,1,64,1,64]{5,3,1,4,2,0:T(8,128)S(1)}, s32[]{:T(128)}) while((s32[]{:T(128)}, f32[4,1,64,64,64]{4,3,2,0,1:T(8,128)}, f32[4,64,64]{2,1,0:T(8,128)S(1)}, f32[2,4,1,64,1,64]{5,3,1,4,2,0:T(8,128)S(1)}, s32[]{:T(128)}) %tuple.73), condition=%wide.region_9.10_spmd, body=%wide.region_7.9_spmd.sunk | while | flops 406847232 | bytes 17107016 | solution.py:143
  32.1 7.7 %multiply_reduce_fusion.4 = (f32[4,64]{1,0:T(4,128)S(1)}, f32[4,64,64,64]{3,2,1,0:T(8,128)S(1)}) fusion(f32[4,64,64]{2,1,0:T(8,128)S(1)} %dynamic-slice_bitcast_fusion.3, f32[4,64,64]{2,1,0:T(8,128)S(1)} %get-tuple-element.181, f32[4,1,64,64,64]{4,3,2,0,1:T(8,128)} %get-tuple-element.175), kind=kOutput, calls=%fused_computation.3.clone.1 | convolution fusion | flops 404750080 | bytes 8520704 | tf_op jit(solution)/shard_map/while/body/eval_jaxpr/kpjim,kml->kpjil/dot_general | solution.py:140
  39.8 4.0 %divide_bitcast_fusion.15 = f32[4,1,64,64,64]{4,3,2,0,1:T(8,128)} fusion(f32[4,64,64,64]{3,2,1,0:T(8,128)S(1)} %get-tuple-element.167, f32[4,64]{1,0:T(4,128)S(1)} %get-tuple-element.168, f32[4,64,64]{2,1,0:T(8,128)S(1)} %dynamic-slice_bitcast_fusion.3), kind=kLoop, calls=%fused_computation.2.clone.1 | loop fusion | flops 2097152 | bytes 8455168 | tf_op jit(solution)/shard_map/while/body/eval_jaxpr/div | solution.py:28
  43.8 7.7 %multiply_reduce_fusion.4 = (f32[4,64]{1,0:T(4,128)S(1)}, f32[4,64,64,64]{3,2,1,0:T(8,128)S(1)}) fusion(f32[4,64,64]{2,1,0:T(8,128)S(1)} %dynamic-slice_bitcast_fusion.3, f32[4,64,64]{2,1,0:T(8,128)S(1)} %get-tuple-element.181, f32[4,1,64,64,64]{4,3,2,0,1:T(8,128)} %get-tuple-element.175), kind=kOutput, calls=%fused_computation.3.clone.1 | convolution fusion | flops 404750080 | bytes 8520704 | tf_op jit(solution)/shard_map/while/body/eval_jaxpr/kpjim,kml->kpjil/dot_general | solution.py:140
  51.5 4.0 %divide_bitcast_fusion.15 = f32[4,1,64,64,64]{4,3,2,0,1:T(8,128)} fusion(f32[4,64,64,64]{3,2,1,0:T(8,128)S(1)} %get-tuple-element.167, f32[4,64]{1,0:T(4,128)S(1)} %get-tuple-element.168, f32[4,64,64]{2,1,0:T(8,128)S(1)} %dynamic-slice_bitcast_fusion.3), kind=kLoop, calls=%fused_computation.2.clone.1 | loop fusion | flops 2097152 | bytes 8455168 | tf_op jit(solution)/shard_map/while/body/eval_jaxpr/div | solution.py:28
  55.5 6.4 %fusion.92 = (f32[4,32]{1,0:T(4,128)S(1)}, f32[4,32,64,64]{3,2,1,0:T(8,128)S(1)}) fusion(f32[4,1,64,64,64]{4,3,2,0,1:T(8,128)} %get-tuple-element.27), kind=kOutput, calls=%fused_computation.214 | convolution fusion | flops 201850752 | bytes 6291968 | tf_op jit(solution)/shard_map/...im,...ml->...il/dot_general | solution.py:36
  62.4 1.4 fusion.93
  66.4 2.8 %all-gather = f32[8,64,64]{2,1,0:T(8,128)S(1)} all-gather(f32[4,64,64]{2,1,0:T(8,128)S(1)} %broadcast_divide_fusion.3), channel_id=2, replica_groups=mesh['people'=2,'tz'=8,'ty'=4,'tc'=2,'type'=2] {'tc'}, dimensions={0}, use_global_device_ids=true | all-gather | bytes 196608 | tf_op jit(solution)/shard_map/all_gather | solution.py:63
  69.9 15.0 %all-gather.1 = f32[4,1,4,1,64,64]{5,4,3,2,1,0:T(8,128)S(1)} all-gather(f32[1,1,4,1,64,64]{5,4,3,2,1,0:T(8,128)S(1)} %get-tuple-element.88), channel_id=3, replica_groups=mesh['people'=2,'tz'=8,'ty'=4,'tc'=2,'type'=2] {'ty'}, dimensions={0}, use_global_device_ids=true | all-gather | bytes 327680 | tf_op jit(solution)/shard_map/all_gather | solution.py:63
  86.3 30.7 %all-gather.2 = f32[8,1,4,1,64,64]{5,4,3,2,1,0:T(8,128)S(1)} all-gather(f32[1,1,4,1,64,64]{5,4,3,2,1,0:T(8,128)S(1)} %get-tuple-element.86), channel_id=4, replica_groups=mesh['people'=2,'tz'=8,'ty'=4,'tc'=2,'type'=2] {'tz'}, dimensions={0}, use_global_device_ids=true | all-gather | bytes 589824 | tf_op jit(solution)/shard_map/all_gather | solution.py:63
  124.8 1.6 fusion.29
  129.0 2.5 %fusion.20 = f32[4,16,1,64]{3,2,1,0:T(1,128)S(1)} fusion(f32[4,16,64,1]{2,3,1,0:T(1,128)S(1)} %bitcast.443, f32[4,1,32,64,64]{4,3,2,0,1:T(8,128)} %copy-done.2), kind=kOutput, calls=%fused_computation.31 | convolution fusion | flops 1572864 | bytes 2129920 | tf_op jit(solution)/shard_map/kpni,kpnil->kpnl/dot_general | solution.py:158
  131.8 1.3 concatenate.46
  133.2 2.9 %fusion.13 = f32[4,32,64]{2,1,0:T(8,128)S(1)} fusion(f32[4,1,64,64,64]{4,3,2,0,1:T(8,128)} %get-tuple-element.27, f32[4,32,64]{2,1,0:T(8,128)S(1)} %copy.258), kind=kLoop, calls=%fused_computation.20 | loop fusion | flops 1040384 | bytes 2162688
  136.8 5.9 %multiply_reduce_fusion.1 = f32[4,64,64]{2,1,0:T(8,128)S(1)} fusion(f32[4,64,64]{2,1,0:T(8,128)S(1)} %copy.259, f32[4,64]{1,0:T(4,128)S(1)} %get-tuple-element.102, f32[4,64,64,64]{3,2,1,0:T(8,128)} %copy-done.1, f32[4,64,64]{2,1,0:T(8,128)S(1)} %get-tuple-element.79), kind=kLoop, calls=%fused_computation.11 | loop fusion | flops 4177920 | bytes 4391936
  146.2 3.9 %psum.28 = f32[2,2,261]{0,2,1:T(8,128)S(1)} all-reduce(f32[2,2,261]{0,2,1:T(8,128)S(1)} %broadcast_multiply_fusion), channel_id=1, replica_groups=mesh['people'=2,'tz'=8,'ty'=4,'tc'=2,'type'=2] {'tc'}, use_global_device_ids=true, to_apply=%region_37.38 | all-reduce | flops 1044 | bytes 8352 | tf_op jit(solution)/shard_map/psum | solution.py:184
  150.1 20.8 %psum.29 = f32[2,2,261]{0,2,1:T(8,128)S(1)} all-reduce(f32[2,2,261]{0,2,1:T(8,128)S(1)} %psum.28), channel_id=1, replica_groups=mesh['people'=2,'tz'=8,'ty'=4,'tc'=2,'type'=2] {'ty'}, use_global_device_ids=true, to_apply=%region_38.39 | all-reduce | flops 1044 | bytes 8352 | tf_op jit(solution)/shard_map/psum | solution.py:184
  170.9 31.5 %psum.30 = f32[2,2,261]{0,2,1:T(8,128)S(1)} all-reduce(f32[2,2,261]{0,2,1:T(8,128)S(1)} %psum.29), channel_id=1, replica_groups=mesh['people'=2,'tz'=8,'ty'=4,'tc'=2,'type'=2] {'tz'}, use_global_device_ids=true, to_apply=%region_39.40 | all-reduce | flops 1044 | bytes 8352 | tf_op jit(solution)/shard_map/psum | solution.py:184
  202.4 18.1 %psum.31 = f32[2,2,261]{0,2,1:T(8,128)S(1)} all-reduce(f32[2,2,261]{0,2,1:T(8,128)S(1)} %psum.30), channel_id=1, replica_groups=mesh['people'=2,'tz'=8,'ty'=4,'tc'=2,'type'=2] {'people','type'}, use_global_device_ids=true, to_apply=%region_40.41 | all-reduce | flops 1044 | bytes 8352 | tf_op jit(solution)/shard_map/psum | solution.py:184
  (167 shorter events, 38.8 us)
Async XLA Ops:
  0.6 17.9 %copy-start = (bf16[3,128,128]{2,1,0:T(8,128)(2,1)S(1)}, bf16[3,128,128]{2,1,0:T(8,128)(2,1)}, u32[]{:S(2)}) copy-start(bf16[3,128,128]{2,1,0:T(8,128)(2,1)} %param.20) | copy-start | bytes 294916
  1.5 15.1 %collective-permute-start.1 = (bf16[3,1,5]{2,0,1:T(4,128)(2,1)S(1)}, bf16[3,1,5]{2,0,1:T(4,128)(2,1)S(1)}, u32[]{:S(2)}, u32[]{:S(2)}) collective-permute-start(bf16[3,1,5]{2,0,1:T(4,128)(2,1)S(1)} %get-tuple-element.97), channel_id=1, source_target_pairs={{2,0},{4,2},{6,4},{8,6},{10,8},{12,10},{14,12},{16,14},{18,16},{20... | collective-permute-start | bytes 98 | tf_op jit(solution)/shard_map/ppermute | solution.py:22
  2.7 13.9 %collective-permute-start = (bf16[3,1,5]{2,0,1:T(4,128)(2,1)S(1)}, bf16[3,1,5]{2,0,1:T(4,128)(2,1)S(1)}, u32[]{:S(2)}, u32[]{:S(2)}) collective-permute-start(bf16[3,1,5]{2,0,1:T(4,128)(2,1)S(1)} %get-tuple-element.96), channel_id=1, source_target_pairs={{0,2},{2,4},{4,6},{6,8},{8,10},{10,12},{12,14},{14,16},{16,18},{18... | collective-permute-start | bytes 98 | tf_op jit(solution)/shard_map/ppermute | solution.py:19
  26.3 5.7 %copy-start.1 = (f32[4,64,64,64]{3,2,1,0:T(8,128)}, f32[4,64,64,64]{3,2,1,0:T(8,128)S(1)}, u32[]{:S(2)}) copy-start(f32[4,64,64,64]{3,2,1,0:T(8,128)S(1)} %get-tuple-element.103) | copy-start | bytes 12582916
  62.4 3.0 %copy-start.2 = (f32[4,1,32,64,64]{4,3,2,0,1:T(8,128)}, f32[4,1,32,64,64]{4,3,2,0,1:T(8,128)S(1)}, u32[]{:S(2)}) copy-start(f32[4,1,32,64,64]{4,3,2,0,1:T(8,128)S(1)} %divide_bitcast_fusion.1) | copy-start | bytes 6291460
  63.8 5.5 %copy-start.13 = (pred[2]{0:T(512)(128)(4,1)S(1)}, pred[2]{0:T(512)(128)(4,1)}, u32[]{:S(2)}) copy-start(pred[2]{0:T(512)(128)(4,1)} %iota_compare_fusion.1) | copy-start | bytes 10
  63.8 21.2 %copy-start.12 = (pred[4]{0:T(512)(128)(4,1)S(1)}, pred[4]{0:T(512)(128)(4,1)}, u32[]{:S(2)}) copy-start(pred[4]{0:T(512)(128)(4,1)} %iota_compare_fusion.2) | copy-start | bytes 16
  65.4 51.6 %copy-start.11 = (pred[8]{0:T(512)(128)(4,1)S(1)}, pred[8]{0:T(512)(128)(4,1)}, u32[]{:S(2)}) copy-start(pred[8]{0:T(512)(128)(4,1)} %iota_compare_fusion.3) | copy-start | bytes 28
  65.6 4.3 %copy-start.3 = (f32[4,1,4,64,64]{4,3,2,0,1:T(8,128)}, f32[4,1,4,64,64]{4,3,2,0,1:T(8,128)S(1)}, u32[]{:S(2)}) copy-start(f32[4,1,4,64,64]{4,3,2,0,1:T(8,128)S(1)} %divide_bitcast_fusion.5) | copy-start | bytes 786436
  66.0 3.3 %copy-start.7 = (f32[4,1,2,64,64]{4,3,2,0,1:T(8,128)}, f32[4,1,2,64,64]{4,3,2,0,1:T(8,128)S(1)}, u32[]{:S(2)}) copy-start(f32[4,1,2,64,64]{4,3,2,0,1:T(8,128)S(1)} %divide_bitcast_fusion.9) | copy-start | bytes 393220
  85.1 34.3 %copy-start.10 = (f32[4,64]{1,0:T(4,128)S(1)}, f32[4,64]{1,0:T(4,128)}, u32[]{:S(2)}) copy-start(f32[4,64]{1,0:T(4,128)} %fusion.79) | copy-start | bytes 3076
  127.7 8.6 %copy-start.4 = (f32[4,1,1,64]{2,3,0,1:T(8,128)S(1)}, f32[4,1,1,64]{2,3,0,1:T(8,128)}, u32[]{:S(2)}) copy-start(f32[4,1,1,64]{2,3,0,1:T(8,128)} %copy.204) | copy-start | bytes 3076
  127.7 8.6 %copy-start.5 = (f32[4,1,1,64]{2,3,0,1:T(8,128)S(1)}, f32[4,1,1,64]{2,3,0,1:T(8,128)}, u32[]{:S(2)}) copy-start(f32[4,1,1,64]{2,3,0,1:T(8,128)} %copy.205) | copy-start | bytes 3076
  127.7 8.6 %copy-start.6 = (f32[4,1,2,64]{2,3,0,1:T(8,128)S(1)}, f32[4,1,2,64]{2,3,0,1:T(8,128)}, u32[]{:S(2)}) copy-start(f32[4,1,2,64]{2,3,0,1:T(8,128)} %fusion.29) | copy-start | bytes 6148
  131.6 11.3 %copy-start.9 = (f32[4,1,128,64]{3,2,0,1:T(8,128)S(1)}, f32[4,1,128,64]{3,2,0,1:T(8,128)}, u32[]{:S(2)}) copy-start(f32[4,1,128,64]{3,2,0,1:T(8,128)} %get-tuple-element.82) | copy-start | bytes 393220
  131.8 11.3 %copy-start.8 = (f32[4,1,128,64]{3,2,0,1:T(8,128)S(1)}, f32[4,1,128,64]{3,2,0,1:T(8,128)}, u32[]{:S(2)}) copy-start(f32[4,1,128,64]{3,2,0,1:T(8,128)} %get-tuple-element.81) | copy-start | bytes 393220
  136.8 84.0 %copy-start.14 = (f32[8]{0:T(128)S(1)}, f32[8]{0:T(128)}, u32[]{:S(2)}) copy-start(f32[8]{0:T(128)} %param.25) | copy-start | bytes 100

commit v2 on v1

--- a/solution.py
+++ b/solution.py
@@ -136,11 +136,8 @@
     cols = [order[:, :, m * quarter : (m + 1) * quarter, None, :] for m in range(4)]
     left = trans[:, None, None] * cols[0]
     pair = norm_mat(jnp.einsum("kpjim,kml->kpjil", left, trans, precision=HIGH) * cols[2])
-    def extend(carry, col):
-        grown = jnp.einsum("kpjim,kml->kpjil", carry, trans, precision=HIGH) * col
-        return norm_mat(grown), None
-
-    level, _ = lax.scan(extend, pair, jnp.stack([cols[1], cols[3]]))
+    level = norm_mat(jnp.einsum("kpjim,kml->kpjil", pair, trans, precision=HIGH) * cols[1])
+    level = norm_mat(jnp.einsum("kpjim,kml->kpjil", level, trans, precision=HIGH) * cols[3])
     levels = [None, pair, level]
     while levels[-1].shape[2] > 1:
         last = levels[-1]
@@ -194,8 +191,8 @@
     occ_all = jnp.take(table, type_index, axis=1)[:, kinds : kinds + kinds * states]
     occ_all = occ_all.reshape(people_n, kinds, states)
     cnt_all = jnp.take(table, type_index, axis=1)[:, kinds + kinds * states]
-    numer = jnp.einsum("pk,pks->ks", post_type, occ_all, precision=HIGHEST)
-    denom = jnp.einsum("pk,p->k", post_type, cnt_all, precision=HIGHEST)
+    numer = jnp.einsum("pk,pks->ks", post_type, occ_all, precision=HIGH)
+    denom = jnp.einsum("pk,p->k", post_type, cnt_all, precision=HIGH)
     occupancy = numer / denom[:, None]
     return (rate_own, post_own, occupancy, filtered)
 

time: 225 us -> 202 us (0.90)
  other arithmetic: 38.9 us -> 25.8 us
  matrix products: 41.6 us -> 33.4 us
    div x14 -> x12, other arithmetic: 14.2 us -> 3.3 us  [norm_mat(): return m / jnp.sum(m, axis=(-2, -1), keepdims=True)]
    dot_general x4, matrix products: 15.9 us -> 10.7 us  [the longest x1 5.28 us: on_device(): jnp.einsum('kpjim,kml->kpjil', level, trans, precision=HIGH) * cols[3]]
    dot_general x14, matrix products: 12.6 us -> 9.26 us  [mat_mat(): return jnp.einsum('...im,...ml->...il', a, b, precision=HIGH)]
where the time goes in v2:
time: 202 us; the launch traced here: 201 us
  blocking collectives  123 us (61%)
  matrix products  33.4 us (17%)
  other arithmetic  25.8 us (13%)
  local copies, waits for them, and re-layouts  12.1 us (6%)
  starting transfers between devices  4.31 us (2%)
  between operations  2.79 us (1%)
    psum x4, blocking collectives, on_device(): table = lax.psum(table, axis)  74.2 us
    all_gather x3, blocking collectives, group_scan(): everyone = lax.all_gather(mats, axis)  48.6 us
    dot_general x14, matrix products, mat_mat(): return jnp.einsum('...im,...ml->...il', a, b, precision=HIGH)  9.26 us
    unnamed x2, other arithmetic  8.83 us
    dot_general x5, matrix products, on_device(): jnp.einsum('kpni,kpnil->kpnl', entry, sibling, precision=HIGH)  5.62 us
    dot_general x1, matrix products, on_device(): jnp.einsum('kpjim,kml->kpjil', level, trans, precision=HIGH) * cols[3]  5.28 us
    dot_general x1, matrix products, on_device(): jnp.einsum('kpjim,kml->kpjil', pair, trans, precision=HIGH) * cols[1]  5.06 us
    dot_general x1, matrix products, on_device(): jnp.einsum('kpjim,kml->kpjil', left, trans, precision=HIGH) * cols[2]  4.56 us
  transfers between devices with their start and end apart: 2, of which 0 were waited for; matrix products, arithmetic and copies ran while one was open for 4% of the time, Pallas kernels for 0%

profile of v2, /device:TPU:4, one launch (start us, length us, event | category | flops | bytes accessed | tf_op | source)
XLA Modules:
  0.0 201.3 jit_solution(12029968872955583317)
XLA Ops:
  1.5 1.3 collective-permute-start.1
  2.7 3.0 %collective-permute-start = (bf16[3,1,5]{2,0,1:T(4,128)(2,1)S(1)}, bf16[3,1,5]{2,0,1:T(4,128)(2,1)S(1)}, u32[]{:S(2)}, u32[]{:S(2)}) collective-permute-start(bf16[3,1,5]{2,0,1:T(4,128)(2,1)S(1)} %get-tuple-element.59), channel_id=1, source_target_pairs={{0,2},{2,4},{4,6},{6,8},{8,10},{10,12},{12,14},{14,16},{16,18},{18... | collective-permute-start | bytes 98 | tf_op jit(solution)/shard_map/ppermute | solution.py:19
  9.2 1.2 fusion.90
  16.4 1.3 bitcast_reduce_fusion
  19.9 4.6 %multiply_reduce_fusion.3 = (f32[4,64]{1,0:T(4,128)S(1)}, f32[4,64,64,64]{3,2,1,0:T(8,128)S(1)}) fusion(f32[4,64,64]{2,1,0:T(8,128)S(1)} %get-tuple-element.42, f32[4,64,64]{2,1,0:T(8,128)S(1)} %multiply_add_fusion, f32[4,64,64]{2,1,0:T(8,128)S(1)} %get-tuple-element.43), kind=kOutput, calls=%fused_computation.15 | convolution fusion | flops 405798656 | bytes 4391936 | tf_op jit(solution)/shard_map/kpjim,kml->kpjil/dot_general | solution.py:138
  24.5 5.1 %multiply_reduce_fusion.2 = (f32[4,64]{1,0:T(4,128)S(1)}, f32[4,64,64,64]{3,2,1,0:T(8,128)S(1)}) fusion(f32[4,64,64]{2,1,0:T(8,128)S(1)} %get-tuple-element.41, f32[4,64,64]{2,1,0:T(8,128)S(1)} %multiply_add_fusion, f32[4,64,64,64]{3,2,1,0:T(8,128)S(1)} %get-tuple-element.66, f32[4,64]{1,0:T(4,128)S(1)} %get-tuple-element.65, ...), kind=kOutput, calls=%fused_computation.13 | convolution fusion | flops 406847232 | bytes 8587264 | tf_op jit(solution)/shard_map/kpjim,kml->kpjil/dot_general | solution.py:139
  29.6 5.3 %multiply_reduce_fusion.1 = (f32[4,64]{1,0:T(4,128)S(1)}, f32[4,64,64,64]{3,2,1,0:T(8,128)S(1)}) fusion(f32[4,64,64]{2,1,0:T(8,128)S(1)} %get-tuple-element.40, f32[4,64,64]{2,1,0:T(8,128)S(1)} %multiply_add_fusion, f32[4,64,64,64]{3,2,1,0:T(8,128)S(1)} %get-tuple-element.68, f32[4,64]{1,0:T(4,128)S(1)} %get-tuple-element.67, ...), kind=kOutput, calls=%fused_computation.11 | convolution fusion | flops 406847232 | bytes 8587264 | tf_op jit(solution)/shard_map/kpjim,kml->kpjil/dot_general | solution.py:140
  34.8 1.7 divide_bitcast_fusion
  36.5 3.1 %fusion.91 = (f32[4,32]{1,0:T(4,128)S(1)}, f32[4,32,64,64]{3,2,1,0:T(8,128)S(1)}) fusion(f32[4,1,64,64,64]{4,3,2,0,1:T(8,128)S(1)} %divide_bitcast_fusion), kind=kOutput, calls=%fused_computation.214 | convolution fusion | flops 201850752 | bytes 6291968 | tf_op jit(solution)/shard_map/...im,...ml->...il/dot_general | solution.py:36
  40.1 1.4 fusion.92
  44.1 2.8 %all-gather = f32[8,64,64]{2,1,0:T(8,128)S(1)} all-gather(f32[4,64,64]{2,1,0:T(8,128)S(1)} %broadcast_divide_fusion.3), channel_id=2, replica_groups=mesh['people'=2,'tz'=8,'ty'=4,'tc'=2,'type'=2] {'tc'}, dimensions={0}, use_global_device_ids=true | all-gather | bytes 196608 | tf_op jit(solution)/shard_map/all_gather | solution.py:63
  47.6 15.3 %all-gather.1 = f32[4,1,4,1,64,64]{5,4,3,2,1,0:T(8,128)S(1)} all-gather(f32[1,1,4,1,64,64]{5,4,3,2,1,0:T(8,128)S(1)} %get-tuple-element.51), channel_id=3, replica_groups=mesh['people'=2,'tz'=8,'ty'=4,'tc'=2,'type'=2] {'ty'}, dimensions={0}, use_global_device_ids=true | all-gather | bytes 327680 | tf_op jit(solution)/shard_map/all_gather | solution.py:63
  64.2 30.5 %all-gather.2 = f32[8,1,4,1,64,64]{5,4,3,2,1,0:T(8,128)S(1)} all-gather(f32[1,1,4,1,64,64]{5,4,3,2,1,0:T(8,128)S(1)} %get-tuple-element.49), channel_id=4, replica_groups=mesh['people'=2,'tz'=8,'ty'=4,'tc'=2,'type'=2] {'tz'}, dimensions={0}, use_global_device_ids=true | all-gather | bytes 589824 | tf_op jit(solution)/shard_map/all_gather | solution.py:63
  97.8 1.1 fusion.63
  99.9 1.2 fusion.41
  101.8 1.6 fusion.26
  106.1 2.5 %fusion.17 = f32[4,16,1,64]{3,2,1,0:T(1,128)S(1)} fusion(f32[4,16,64,1]{2,3,1,0:T(1,128)S(1)} %bitcast.426, f32[4,1,32,64,64]{4,3,2,0,1:T(8,128)} %copy-done.4), kind=kOutput, calls=%fused_computation.30 | convolution fusion | flops 1572864 | bytes 2129920 | tf_op jit(solution)/shard_map/kpni,kpnil->kpnl/dot_general | solution.py:155
  108.8 1.3 concatenate.46
  110.2 2.9 %multiply_reduce_fusion.4 = f32[4,32,64]{2,1,0:T(8,128)S(1)} fusion(f32[4,1,64,64,64]{4,3,2,0,1:T(8,128)} %copy-done.2, f32[4,32,64]{2,1,0:T(8,128)S(1)} %copy.258), kind=kLoop, calls=%fused_computation.19 | loop fusion | flops 1040384 | bytes 2162688
  113.8 5.9 %multiply_reduce_fusion = f32[4,64,64]{2,1,0:T(8,128)S(1)} fusion(f32[4,64,64]{2,1,0:T(8,128)S(1)} %copy.259, f32[4,64]{1,0:T(4,128)S(1)} %get-tuple-element.65, f32[4,64,64,64]{3,2,1,0:T(8,128)} %copy-done.3, f32[4,64,64]{2,1,0:T(8,128)} %copy-done.9), kind=kLoop, calls=%fused_computation.5 | loop fusion | flops 4177920 | bytes 4391936
  123.2 3.9 %psum.28 = f32[2,2,261]{0,2,1:T(8,128)S(1)} all-reduce(f32[2,2,261]{0,2,1:T(8,128)S(1)} %broadcast_multiply_fusion), channel_id=1, replica_groups=mesh['people'=2,'tz'=8,'ty'=4,'tc'=2,'type'=2] {'tc'}, use_global_device_ids=true, to_apply=%region_36.37 | all-reduce | flops 1044 | bytes 8352 | tf_op jit(solution)/shard_map/psum | solution.py:181
  127.1 20.8 %psum.29 = f32[2,2,261]{0,2,1:T(8,128)S(1)} all-reduce(f32[2,2,261]{0,2,1:T(8,128)S(1)} %psum.28), channel_id=1, replica_groups=mesh['people'=2,'tz'=8,'ty'=4,'tc'=2,'type'=2] {'ty'}, use_global_device_ids=true, to_apply=%region_37.38 | all-reduce | flops 1044 | bytes 8352 | tf_op jit(solution)/shard_map/psum | solution.py:181
  147.9 31.5 %psum.30 = f32[2,2,261]{0,2,1:T(8,128)S(1)} all-reduce(f32[2,2,261]{0,2,1:T(8,128)S(1)} %psum.29), channel_id=1, replica_groups=mesh['people'=2,'tz'=8,'ty'=4,'tc'=2,'type'=2] {'tz'}, use_global_device_ids=true, to_apply=%region_38.39 | all-reduce | flops 1044 | bytes 8352 | tf_op jit(solution)/shard_map/psum | solution.py:181
  179.4 18.1 %psum.31 = f32[2,2,261]{0,2,1:T(8,128)S(1)} all-reduce(f32[2,2,261]{0,2,1:T(8,128)S(1)} %psum.30), channel_id=1, replica_groups=mesh['people'=2,'tz'=8,'ty'=4,'tc'=2,'type'=2] {'people','type'}, use_global_device_ids=true, to_apply=%region_39.40 | all-reduce | flops 1044 | bytes 8352 | tf_op jit(solution)/shard_map/psum | solution.py:181
  (157 shorter events, 31.4 us)
Async XLA Ops:
  0.6 15.7 %copy-start = (bf16[3,128,128]{2,1,0:T(8,128)(2,1)S(1)}, bf16[3,128,128]{2,1,0:T(8,128)(2,1)}, u32[]{:S(2)}) copy-start(bf16[3,128,128]{2,1,0:T(8,128)(2,1)} %param.18) | copy-start | bytes 294916
  1.5 13.0 %collective-permute-start.1 = (bf16[3,1,5]{2,0,1:T(4,128)(2,1)S(1)}, bf16[3,1,5]{2,0,1:T(4,128)(2,1)S(1)}, u32[]{:S(2)}, u32[]{:S(2)}) collective-permute-start(bf16[3,1,5]{2,0,1:T(4,128)(2,1)S(1)} %get-tuple-element.60), channel_id=1, source_target_pairs={{2,0},{4,2},{6,4},{8,6},{10,8},{12,10},{14,12},{16,14},{18,16},{20... | collective-permute-start | bytes 98 | tf_op jit(solution)/shard_map/ppermute | solution.py:22
  2.7 11.7 %collective-permute-start = (bf16[3,1,5]{2,0,1:T(4,128)(2,1)S(1)}, bf16[3,1,5]{2,0,1:T(4,128)(2,1)S(1)}, u32[]{:S(2)}, u32[]{:S(2)}) collective-permute-start(bf16[3,1,5]{2,0,1:T(4,128)(2,1)S(1)} %get-tuple-element.59), channel_id=1, source_target_pairs={{0,2},{2,4},{4,6},{6,8},{8,10},{10,12},{12,14},{14,16},{16,18},{18... | collective-permute-start | bytes 98 | tf_op jit(solution)/shard_map/ppermute | solution.py:19
  19.9 9.6 %copy-start.9 = (f32[4,64,64]{2,1,0:T(8,128)}, f32[4,64,64]{2,1,0:T(8,128)S(1)}, u32[]{:S(2)}) copy-start(f32[4,64,64]{2,1,0:T(8,128)S(1)} %get-tuple-element.42) | copy-start | bytes 196612
  24.5 5.1 %copy-start.3 = (f32[4,64,64,64]{3,2,1,0:T(8,128)}, f32[4,64,64,64]{3,2,1,0:T(8,128)S(1)}, u32[]{:S(2)}) copy-start(f32[4,64,64,64]{3,2,1,0:T(8,128)S(1)} %get-tuple-element.66) | copy-start | bytes 12582916
  36.5 3.6 %copy-start.2 = (f32[4,1,64,64,64]{4,3,2,0,1:T(8,128)}, f32[4,1,64,64,64]{4,3,2,0,1:T(8,128)S(1)}, u32[]{:S(2)}) copy-start(f32[4,1,64,64,64]{4,3,2,0,1:T(8,128)S(1)} %divide_bitcast_fusion) | copy-start | bytes 12582916
  40.1 3.0 %copy-start.4 = (f32[4,1,32,64,64]{4,3,2,0,1:T(8,128)}, f32[4,1,32,64,64]{4,3,2,0,1:T(8,128)S(1)}, u32[]{:S(2)}) copy-start(f32[4,1,32,64,64]{4,3,2,0,1:T(8,128)S(1)} %divide_bitcast_fusion.1) | copy-start | bytes 6291460
  43.3 4.3 %copy-start.5 = (f32[4,1,4,64,64]{4,3,2,0,1:T(8,128)}, f32[4,1,4,64,64]{4,3,2,0,1:T(8,128)S(1)}, u32[]{:S(2)}) copy-start(f32[4,1,4,64,64]{4,3,2,0,1:T(8,128)S(1)} %divide_bitcast_fusion.5) | copy-start | bytes 786436
  43.7 3.3 %copy-start.8 = (f32[4,1,2,64,64]{4,3,2,0,1:T(8,128)}, f32[4,1,2,64,64]{4,3,2,0,1:T(8,128)S(1)}, u32[]{:S(2)}) copy-start(f32[4,1,2,64,64]{4,3,2,0,1:T(8,128)S(1)} %divide_bitcast_fusion.9) | copy-start | bytes 393220
  104.8 8.6 %copy-start.6 = (f32[4,1,1,64]{2,3,0,1:T(8,128)S(1)}, f32[4,1,1,64]{2,3,0,1:T(8,128)}, u32[]{:S(2)}) copy-start(f32[4,1,1,64]{2,3,0,1:T(8,128)} %copy.206) | copy-start | bytes 3076
  104.8 8.6 %copy-start.7 = (f32[4,1,2,64]{2,3,0,1:T(8,128)S(1)}, f32[4,1,2,64]{2,3,0,1:T(8,128)}, u32[]{:S(2)}) copy-start(f32[4,1,2,64]{2,3,0,1:T(8,128)} %fusion.26) | copy-start | bytes 6148
  108.7 11.2 %copy-start.11 = (f32[4,1,128,64]{3,2,0,1:T(8,128)S(1)}, f32[4,1,128,64]{3,2,0,1:T(8,128)}, u32[]{:S(2)}) copy-start(f32[4,1,128,64]{3,2,0,1:T(8,128)} %get-tuple-element.45) | copy-start | bytes 393220
  108.8 11.2 %copy-start.10 = (f32[4,1,128,64]{3,2,0,1:T(8,128)S(1)}, f32[4,1,128,64]{3,2,0,1:T(8,128)}, u32[]{:S(2)}) copy-start(f32[4,1,128,64]{3,2,0,1:T(8,128)} %get-tuple-element.44) | copy-start | bytes 393220
  113.6 87.6 %copy-start.1 = (bf16[3,128,128]{2,1,0:T(8,128)(2,1)S(1)}, bf16[3,128,128]{2,1,0:T(8,128)(2,1)}, u32[]{:S(2)}) copy-start(bf16[3,128,128]{2,1,0:T(8,128)(2,1)} %param.18) | copy-start | bytes 294916
  113.8 84.0 %copy-start.12 = (f32[8]{0:T(128)S(1)}, f32[8]{0:T(128)}, u32[]{:S(2)}) copy-start(f32[8]{0:T(128)} %param.23) | copy-start | bytes 100

commit v3 on v2

--- a/solution.py
+++ b/solution.py
@@ -60,7 +60,7 @@
     count = lax.axis_size(axis)
     mine = lax.axis_index(axis)
     eye = jnp.eye(mats.shape[-1], dtype=mats.dtype)
-    everyone = lax.all_gather(mats, axis)
+    everyone = lax.all_gather(mats.astype(jnp.bfloat16), axis).astype(mats.dtype)
     keep = (jnp.arange(count) < mine).reshape((count,) + (1,) * mats.ndim)
     earlier = jnp.where(keep, everyone, eye)
     if not whole:

time: 202 us -> 200 us (0.990)
  blocking collectives: 123 us -> 120 us
    all_gather x3, blocking collectives: 48.6 us -> 45.9 us  [group_scan(): lax.all_gather(mats.astype(jnp.bfloat16), axis).astype(mats.dtype)]
where the time goes in v3:
time: 200 us; the launch traced here: 199 us
  blocking collectives  120 us (60%)
  matrix products  33.4 us (17%)
  other arithmetic  25.9 us (13%)
  local copies, waits for them, and re-layouts  12.9 us (6%)
  starting transfers between devices  4.31 us (2%)
  between operations  2.81 us (1%)
    psum x4, blocking collectives, on_device(): table = lax.psum(table, axis)  74.2 us
    all_gather x3, blocking collectives, group_scan(): lax.all_gather(mats.astype(jnp.bfloat16), axis).astype(mats.dtype)  45.9 us
    dot_general x14, matrix products, mat_mat(): return jnp.einsum('...im,...ml->...il', a, b, precision=HIGH)  9.26 us
    unnamed x2, other arithmetic  8.83 us
    dot_general x5, matrix products, on_device(): jnp.einsum('kpni,kpnil->kpnl', entry, sibling, precision=HIGH)  5.62 us
    dot_general x1, matrix products, on_device(): jnp.einsum('kpjim,kml->kpjil', level, trans, precision=HIGH) * cols[3]  5.28 us
    dot_general x1, matrix products, on_device(): jnp.einsum('kpjim,kml->kpjil', pair, trans, precision=HIGH) * cols[1]  5.06 us
    dot_general x1, matrix products, on_device(): jnp.einsum('kpjim,kml->kpjil', left, trans, precision=HIGH) * cols[2]  4.56 us
  transfers between devices with their start and end apart: 2, of which 0 were waited for; matrix products, arithmetic and copies ran while one was open for 4% of the time, Pallas kernels for 0%

profile of v3, /device:TPU:4, one launch (start us, length us, event | category | flops | bytes accessed | tf_op | source)
XLA Modules:
  0.0 199.4 jit_solution(12737302268370999908)
XLA Ops:
  1.5 1.3 collective-permute-start.1
  2.7 3.0 %collective-permute-start = (bf16[3,1,5]{2,0,1:T(4,128)(2,1)S(1)}, bf16[3,1,5]{2,0,1:T(4,128)(2,1)S(1)}, u32[]{:S(2)}, u32[]{:S(2)}) collective-permute-start(bf16[3,1,5]{2,0,1:T(4,128)(2,1)S(1)} %get-tuple-element.55), channel_id=1, source_target_pairs={{0,2},{2,4},{4,6},{6,8},{8,10},{10,12},{12,14},{14,16},{16,18},{18... | collective-permute-start | bytes 98 | tf_op jit(solution)/shard_map/ppermute | solution.py:19
  9.2 1.2 fusion.92
  16.4 1.3 bitcast_reduce_fusion
  19.9 4.6 %multiply_reduce_fusion.3 = (f32[4,64]{1,0:T(4,128)S(1)}, f32[4,64,64,64]{3,2,1,0:T(8,128)S(1)}) fusion(f32[4,64,64]{2,1,0:T(8,128)S(1)} %get-tuple-element.42, f32[4,64,64]{2,1,0:T(8,128)S(1)} %multiply_add_fusion, f32[4,64,64]{2,1,0:T(8,128)S(1)} %get-tuple-element.43), kind=kOutput, calls=%fused_computation.15 | convolution fusion | flops 405798656 | bytes 4391936 | tf_op jit(solution)/shard_map/kpjim,kml->kpjil/dot_general | solution.py:138
  24.5 5.1 %multiply_reduce_fusion.2 = (f32[4,64]{1,0:T(4,128)S(1)}, f32[4,64,64,64]{3,2,1,0:T(8,128)S(1)}) fusion(f32[4,64,64]{2,1,0:T(8,128)S(1)} %get-tuple-element.41, f32[4,64,64]{2,1,0:T(8,128)S(1)} %multiply_add_fusion, f32[4,64,64,64]{3,2,1,0:T(8,128)S(1)} %get-tuple-element.62, f32[4,64]{1,0:T(4,128)S(1)} %get-tuple-element.61, ...), kind=kOutput, calls=%fused_computation.13 | convolution fusion | flops 406847232 | bytes 8587264 | tf_op jit(solution)/shard_map/kpjim,kml->kpjil/dot_general | solution.py:139
  29.6 5.3 %multiply_reduce_fusion.1 = (f32[4,64]{1,0:T(4,128)S(1)}, f32[4,64,64,64]{3,2,1,0:T(8,128)S(1)}) fusion(f32[4,64,64]{2,1,0:T(8,128)S(1)} %get-tuple-element.40, f32[4,64,64]{2,1,0:T(8,128)S(1)} %multiply_add_fusion, f32[4,64,64,64]{3,2,1,0:T(8,128)S(1)} %get-tuple-element.64, f32[4,64]{1,0:T(4,128)S(1)} %get-tuple-element.63, ...), kind=kOutput, calls=%fused_computation.11 | convolution fusion | flops 406847232 | bytes 8587264 | tf_op jit(solution)/shard_map/kpjim,kml->kpjil/dot_general | solution.py:140
  34.8 1.7 divide_bitcast_fusion
  36.5 3.1 %fusion.93 = (f32[4,32]{1,0:T(4,128)S(1)}, f32[4,32,64,64]{3,2,1,0:T(8,128)S(1)}) fusion(f32[4,1,64,64,64]{4,3,2,0,1:T(8,128)S(1)} %divide_bitcast_fusion), kind=kOutput, calls=%fused_computation.217 | convolution fusion | flops 201850752 | bytes 6291968 | tf_op jit(solution)/shard_map/...im,...ml->...il/dot_general | solution.py:36
  40.1 1.4 fusion.94
  44.9 2.7 %all-gather = bf16[8,64,64]{2,1,0:T(8,128)(2,1)S(1)} all-gather(bf16[4,64,64]{2,1,0:T(8,128)(2,1)S(1)} %divide_convert_fusion), channel_id=2, replica_groups=mesh['people'=2,'tz'=8,'ty'=4,'tc'=2,'type'=2] {'tc'}, dimensions={0}, use_global_device_ids=true | all-gather | bytes 98304 | tf_op jit(solution)/shard_map/all_gather | solution.py:63
  48.3 14.3 %all-gather.1 = bf16[4,1,4,1,64,64]{5,4,3,2,1,0:T(8,128)(2,1)S(1)} all-gather(bf16[1,1,4,1,64,64]{5,4,3,2,1,0:T(8,128)(2,1)S(1)} %fusion.64), channel_id=3, replica_groups=mesh['people'=2,'tz'=8,'ty'=4,'tc'=2,'type'=2] {'ty'}, dimensions={0}, use_global_device_ids=true | all-gather | bytes 163840 | tf_op jit(solution)/shard_map/all_gather | solution.py:63
  64.0 28.9 %all-gather.2 = bf16[8,1,4,1,64,64]{5,4,3,2,1,0:T(8,128)(2,1)S(1)} all-gather(bf16[1,1,4,1,64,64]{5,4,3,2,1,0:T(8,128)(2,1)S(1)} %fusion.65), channel_id=4, replica_groups=mesh['people'=2,'tz'=8,'ty'=4,'tc'=2,'type'=2] {'tz'}, dimensions={0}, use_global_device_ids=true | all-gather | bytes 294912 | tf_op jit(solution)/shard_map/all_gather | solution.py:63
  95.9 1.1 fusion.63
  98.1 1.2 fusion.41
  100.0 1.6 fusion.26
  104.2 2.5 %fusion.17 = f32[4,16,1,64]{3,2,1,0:T(1,128)S(1)} fusion(f32[4,16,64,1]{2,3,1,0:T(1,128)S(1)} %bitcast.433, f32[4,1,32,64,64]{4,3,2,0,1:T(8,128)} %copy-done.4), kind=kOutput, calls=%fused_computation.30 | convolution fusion | flops 1572864 | bytes 2129920 | tf_op jit(solution)/shard_map/kpni,kpnil->kpnl/dot_general | solution.py:155
  107.0 1.3 concatenate.46
  108.4 2.9 %multiply_reduce_fusion.4 = f32[4,32,64]{2,1,0:T(8,128)S(1)} fusion(f32[4,1,64,64,64]{4,3,2,0,1:T(8,128)} %copy-done.2, f32[4,32,64]{2,1,0:T(8,128)S(1)} %copy.260), kind=kLoop, calls=%fused_computation.19 | loop fusion | flops 1040384 | bytes 2162688
  112.0 5.9 %multiply_reduce_fusion = f32[4,64,64]{2,1,0:T(8,128)S(1)} fusion(f32[4,64,64]{2,1,0:T(8,128)S(1)} %copy.261, f32[4,64]{1,0:T(4,128)S(1)} %get-tuple-element.61, f32[4,64,64,64]{3,2,1,0:T(8,128)} %copy-done.3, f32[4,64,64]{2,1,0:T(8,128)} %copy-done.9), kind=kLoop, calls=%fused_computation.5 | loop fusion | flops 4177920 | bytes 4391936
  121.4 3.9 %psum.28 = f32[2,2,261]{0,2,1:T(8,128)S(1)} all-reduce(f32[2,2,261]{0,2,1:T(8,128)S(1)} %broadcast_multiply_fusion), channel_id=1, replica_groups=mesh['people'=2,'tz'=8,'ty'=4,'tc'=2,'type'=2] {'tc'}, use_global_device_ids=true, to_apply=%region_36.37 | all-reduce | flops 1044 | bytes 8352 | tf_op jit(solution)/shard_map/psum | solution.py:181
  125.3 20.9 %psum.29 = f32[2,2,261]{0,2,1:T(8,128)S(1)} all-reduce(f32[2,2,261]{0,2,1:T(8,128)S(1)} %psum.28), channel_id=1, replica_groups=mesh['people'=2,'tz'=8,'ty'=4,'tc'=2,'type'=2] {'ty'}, use_global_device_ids=true, to_apply=%region_37.38 | all-reduce | flops 1044 | bytes 8352 | tf_op jit(solution)/shard_map/psum | solution.py:181
  146.2 31.3 %psum.30 = f32[2,2,261]{0,2,1:T(8,128)S(1)} all-reduce(f32[2,2,261]{0,2,1:T(8,128)S(1)} %psum.29), channel_id=1, replica_groups=mesh['people'=2,'tz'=8,'ty'=4,'tc'=2,'type'=2] {'tz'}, use_global_device_ids=true, to_apply=%region_38.39 | all-reduce | flops 1044 | bytes 8352 | tf_op jit(solution)/shard_map/psum | solution.py:181
  177.5 18.1 %psum.31 = f32[2,2,261]{0,2,1:T(8,128)S(1)} all-reduce(f32[2,2,261]{0,2,1:T(8,128)S(1)} %psum.30), channel_id=1, replica_groups=mesh['people'=2,'tz'=8,'ty'=4,'tc'=2,'type'=2] {'people','type'}, use_global_device_ids=true, to_apply=%region_39.40 | all-reduce | flops 1044 | bytes 8352 | tf_op jit(solution)/shard_map/psum | solution.py:181
  (161 shorter events, 32.2 us)
Async XLA Ops:
  0.6 15.7 %copy-start = (bf16[3,128,128]{2,1,0:T(8,128)(2,1)S(1)}, bf16[3,128,128]{2,1,0:T(8,128)(2,1)}, u32[]{:S(2)}) copy-start(bf16[3,128,128]{2,1,0:T(8,128)(2,1)} %param.18) | copy-start | bytes 294916
  1.5 13.0 %collective-permute-start.1 = (bf16[3,1,5]{2,0,1:T(4,128)(2,1)S(1)}, bf16[3,1,5]{2,0,1:T(4,128)(2,1)S(1)}, u32[]{:S(2)}, u32[]{:S(2)}) collective-permute-start(bf16[3,1,5]{2,0,1:T(4,128)(2,1)S(1)} %get-tuple-element.56), channel_id=1, source_target_pairs={{2,0},{4,2},{6,4},{8,6},{10,8},{12,10},{14,12},{16,14},{18,16},{20... | collective-permute-start | bytes 98 | tf_op jit(solution)/shard_map/ppermute | solution.py:22
  2.7 11.7 %collective-permute-start = (bf16[3,1,5]{2,0,1:T(4,128)(2,1)S(1)}, bf16[3,1,5]{2,0,1:T(4,128)(2,1)S(1)}, u32[]{:S(2)}, u32[]{:S(2)}) collective-permute-start(bf16[3,1,5]{2,0,1:T(4,128)(2,1)S(1)} %get-tuple-element.55), channel_id=1, source_target_pairs={{0,2},{2,4},{4,6},{6,8},{8,10},{10,12},{12,14},{14,16},{16,18},{18... | collective-permute-start | bytes 98 | tf_op jit(solution)/shard_map/ppermute | solution.py:19
  19.9 9.6 %copy-start.9 = (f32[4,64,64]{2,1,0:T(8,128)}, f32[4,64,64]{2,1,0:T(8,128)S(1)}, u32[]{:S(2)}) copy-start(f32[4,64,64]{2,1,0:T(8,128)S(1)} %get-tuple-element.42) | copy-start | bytes 196612
  24.5 5.1 %copy-start.3 = (f32[4,64,64,64]{3,2,1,0:T(8,128)}, f32[4,64,64,64]{3,2,1,0:T(8,128)S(1)}, u32[]{:S(2)}) copy-start(f32[4,64,64,64]{3,2,1,0:T(8,128)S(1)} %get-tuple-element.62) | copy-start | bytes 12582916
  36.5 3.6 %copy-start.2 = (f32[4,1,64,64,64]{4,3,2,0,1:T(8,128)}, f32[4,1,64,64,64]{4,3,2,0,1:T(8,128)S(1)}, u32[]{:S(2)}) copy-start(f32[4,1,64,64,64]{4,3,2,0,1:T(8,128)S(1)} %divide_bitcast_fusion) | copy-start | bytes 12582916
  40.1 3.0 %copy-start.4 = (f32[4,1,32,64,64]{4,3,2,0,1:T(8,128)}, f32[4,1,32,64,64]{4,3,2,0,1:T(8,128)S(1)}, u32[]{:S(2)}) copy-start(f32[4,1,32,64,64]{4,3,2,0,1:T(8,128)S(1)} %divide_bitcast_fusion.1) | copy-start | bytes 6291460
  43.3 0.8 copy-start.5
  44.5 3.3 %copy-start.8 = (f32[4,1,2,64,64]{4,3,2,0,1:T(8,128)}, f32[4,1,2,64,64]{4,3,2,0,1:T(8,128)S(1)}, u32[]{:S(2)}) copy-start(f32[4,1,2,64,64]{4,3,2,0,1:T(8,128)S(1)} %divide_bitcast_fusion.9) | copy-start | bytes 393220
  103.0 8.6 %copy-start.6 = (f32[4,1,1,64]{2,3,0,1:T(8,128)S(1)}, f32[4,1,1,64]{2,3,0,1:T(8,128)}, u32[]{:S(2)}) copy-start(f32[4,1,1,64]{2,3,0,1:T(8,128)} %copy.208) | copy-start | bytes 3076
  103.0 8.6 %copy-start.7 = (f32[4,1,2,64]{2,3,0,1:T(8,128)S(1)}, f32[4,1,2,64]{2,3,0,1:T(8,128)}, u32[]{:S(2)}) copy-start(f32[4,1,2,64]{2,3,0,1:T(8,128)} %fusion.26) | copy-start | bytes 6148
  106.9 11.2 %copy-start.11 = (f32[4,1,128,64]{3,2,0,1:T(8,128)S(1)}, f32[4,1,128,64]{3,2,0,1:T(8,128)}, u32[]{:S(2)}) copy-start(f32[4,1,128,64]{3,2,0,1:T(8,128)} %get-tuple-element.45) | copy-start | bytes 393220
  107.0 11.2 %copy-start.10 = (f32[4,1,128,64]{3,2,0,1:T(8,128)S(1)}, f32[4,1,128,64]{3,2,0,1:T(8,128)}, u32[]{:S(2)}) copy-start(f32[4,1,128,64]{3,2,0,1:T(8,128)} %get-tuple-element.44) | copy-start | bytes 393220
  111.8 87.6 %copy-start.1 = (bf16[3,128,128]{2,1,0:T(8,128)(2,1)S(1)}, bf16[3,128,128]{2,1,0:T(8,128)(2,1)}, u32[]{:S(2)}) copy-start(bf16[3,128,128]{2,1,0:T(8,128)(2,1)} %param.18) | copy-start | bytes 294916
  111.9 84.0 %copy-start.12 = (f32[8]{0:T(128)S(1)}, f32[8]{0:T(128)}, u32[]{:S(2)}) copy-start(f32[8]{0:T(128)} %param.23) | copy-start | bytes 100

commit v4 on v3

--- a/solution.py
+++ b/solution.py
@@ -152,7 +152,7 @@
     for depth in range(len(levels) - 1, 1, -1):
         n = entry.shape[2]
         sibling = levels[depth - 1][:, :, :n]
-        moved = norm_vec(jnp.einsum("kpni,kpnil->kpnl", entry, sibling, precision=HIGH))
+        moved = norm_vec(jnp.sum(entry[..., :, None] * sibling, axis=-2))
         entry = jnp.concatenate([entry, moved], axis=2)
     u = jnp.einsum("kpji,kil->kpjl", entry, trans, precision=HIGH) * e_even
     c_even = jnp.sum(u, axis=-1)
@@ -163,7 +163,7 @@
     alpha = bit_reverse(jnp.concatenate([a_even, a_odd], axis=2), 2)
     filtered = jnp.transpose(alpha, (1, 2, 0, 3))
     own_log = jnp.transpose(jnp.sum(jnp.log(c_even), axis=2) + jnp.sum(jnp.log(c_odd), axis=2))
-    occupied = jnp.einsum("pt,ptks->pks", observed_f, filtered, precision=HIGH)
+    occupied = jnp.sum(observed_f[:, :, None, None] * filtered, axis=1)
     count = jnp.sum(observed_f, axis=1)
 
     halves_n = lax.axis_size("type")
@@ -191,8 +191,8 @@
     occ_all = jnp.take(table, type_index, axis=1)[:, kinds : kinds + kinds * states]
     occ_all = occ_all.reshape(people_n, kinds, states)
     cnt_all = jnp.take(table, type_index, axis=1)[:, kinds + kinds * states]
-    numer = jnp.einsum("pk,pks->ks", post_type, occ_all, precision=HIGH)
-    denom = jnp.einsum("pk,p->k", post_type, cnt_all, precision=HIGH)
+    numer = jnp.sum(post_type[:, :, None] * occ_all, axis=0)
+    denom = jnp.sum(post_type * cnt_all[:, None], axis=0)
     occupancy = numer / denom[:, None]
     return (rate_own, post_own, occupancy, filtered)
 

time: 200 us -> 205 us (1.025)
  other arithmetic: 25.9 us -> 34.1 us
  matrix products: 33.4 us -> 27.2 us
  local copies, waits for them, and re-layouts: 12.9 us -> 15.7 us
    reduce_sum x4 -> x8, other arithmetic: 0.44 us -> 18.2 us  [norm_vec(): return v / jnp.sum(v, axis=-1, keepdims=True)]
    unnamed x2 -> x0, other arithmetic: 8.83 us -> none
    dot_general x8 -> x0, matrix products: 6.16 us -> none  [the longest x5 5.62 us: on_device(): jnp.einsum('kpni,kpnil->kpnl', entry, sibling, precision=HIGH)]
    unnamed x32 -> x30, local copies, waits for them, and re-layouts: 2.74 us -> 5.78 us
where the time goes in v4:
time: 205 us; the launch traced here: 204 us
  blocking collectives  120 us (59%)
  other arithmetic  34.1 us (17%)
  matrix products  27.2 us (13%)
  local copies, waits for them, and re-layouts  15.7 us (8%)
  starting transfers between devices  4.31 us (2%)
  between operations  2.75 us (1%)
    psum x4, blocking collectives, on_device(): table = lax.psum(table, axis)  74.2 us
    all_gather x3, blocking collectives, group_scan(): lax.all_gather(mats.astype(jnp.bfloat16), axis).astype(mats.dtype)  45.9 us
    reduce_sum x8, other arithmetic, norm_vec(): return v / jnp.sum(v, axis=-1, keepdims=True)  18.2 us
    dot_general x14, matrix products, mat_mat(): return jnp.einsum('...im,...ml->...il', a, b, precision=HIGH)  9.26 us
    unnamed x30, local copies, waits for them, and re-layouts  5.78 us
    dot_general x1, matrix products, on_device(): jnp.einsum('kpjim,kml->kpjil', level, trans, precision=HIGH) * cols[3]  5.27 us
    dot_general x1, matrix products, on_device(): jnp.einsum('kpjim,kml->kpjil', pair, trans, precision=HIGH) * cols[1]  5.06 us
    dot_general x1, matrix products, on_device(): jnp.einsum('kpjim,kml->kpjil', left, trans, precision=HIGH) * cols[2]  4.56 us
  transfers between devices with their start and end apart: 2, of which 0 were waited for; matrix products, arithmetic and copies ran while one was open for 4% of the time, Pallas kernels for 0%

profile of v4, /device:TPU:4, one launch (start us, length us, event | category | flops | bytes accessed | tf_op | source)
XLA Modules:
  0.0 204.2 jit_solution(12436785191550778649)
XLA Ops:
  1.5 1.3 collective-permute-start.1
  2.7 3.0 %collective-permute-start = (bf16[3,1,5]{2,0,1:T(4,128)(2,1)S(1)}, bf16[3,1,5]{2,0,1:T(4,128)(2,1)S(1)}, u32[]{:S(2)}, u32[]{:S(2)}) collective-permute-start(bf16[3,1,5]{2,0,1:T(4,128)(2,1)S(1)} %get-tuple-element.75), channel_id=1, source_target_pairs={{0,2},{2,4},{4,6},{6,8},{8,10},{10,12},{12,14},{14,16},{16,18},{18... | collective-permute-start | bytes 98 | tf_op jit(solution)/shard_map/ppermute | solution.py:19
  9.2 1.2 fusion.90
  16.4 1.3 bitcast_reduce_fusion
  19.9 4.6 %multiply_reduce_fusion.4 = (f32[4,64]{1,0:T(4,128)S(1)}, f32[4,64,64,64]{3,2,1,0:T(8,128)S(1)}) fusion(f32[4,64,64]{2,1,0:T(8,128)S(1)} %get-tuple-element.62, f32[4,64,64]{2,1,0:T(8,128)S(1)} %multiply_add_fusion, f32[4,64,64]{2,1,0:T(8,128)S(1)} %get-tuple-element.63), kind=kOutput, calls=%fused_computation.12 | convolution fusion | flops 405798656 | bytes 4391936 | tf_op jit(solution)/shard_map/kpjim,kml->kpjil/dot_general | solution.py:138
  24.5 5.1 %multiply_reduce_fusion.3 = (f32[4,64]{1,0:T(4,128)S(1)}, f32[4,64,64,64]{3,2,1,0:T(8,128)S(1)}) fusion(f32[4,64,64]{2,1,0:T(8,128)S(1)} %get-tuple-element.61, f32[4,64,64]{2,1,0:T(8,128)S(1)} %multiply_add_fusion, f32[4,64,64,64]{3,2,1,0:T(8,128)S(1)} %get-tuple-element.82, f32[4,64]{1,0:T(4,128)S(1)} %get-tuple-element.81, ...), kind=kOutput, calls=%fused_computation.10 | convolution fusion | flops 406847232 | bytes 8587264 | tf_op jit(solution)/shard_map/kpjim,kml->kpjil/dot_general | solution.py:139
  29.6 5.3 %multiply_reduce_fusion.2 = (f32[4,64]{1,0:T(4,128)S(1)}, f32[4,64,64,64]{3,2,1,0:T(8,128)S(1)}) fusion(f32[4,64,64]{2,1,0:T(8,128)S(1)} %get-tuple-element.60, f32[4,64,64]{2,1,0:T(8,128)S(1)} %multiply_add_fusion, f32[4,64,64,64]{3,2,1,0:T(8,128)S(1)} %get-tuple-element.84, f32[4,64]{1,0:T(4,128)S(1)} %get-tuple-element.83, ...), kind=kOutput, calls=%fused_computation.8 | convolution fusion | flops 406847232 | bytes 8587264 | tf_op jit(solution)/shard_map/kpjim,kml->kpjil/dot_general | solution.py:140
  34.8 1.7 divide_bitcast_fusion
  36.5 3.1 %fusion.91 = (f32[4,32]{1,0:T(4,128)S(1)}, f32[4,32,64,64]{3,2,1,0:T(8,128)S(1)}) fusion(f32[4,1,64,64,64]{4,3,2,0,1:T(8,128)S(1)} %divide_bitcast_fusion), kind=kOutput, calls=%fused_computation.218 | convolution fusion | flops 201850752 | bytes 6291968 | tf_op jit(solution)/shard_map/...im,...ml->...il/dot_general | solution.py:36
  40.1 1.4 fusion.92
  44.9 2.7 %all-gather = bf16[8,64,64]{2,1,0:T(8,128)(2,1)S(1)} all-gather(bf16[4,64,64]{2,1,0:T(8,128)(2,1)S(1)} %divide_convert_fusion), channel_id=2, replica_groups=mesh['people'=2,'tz'=8,'ty'=4,'tc'=2,'type'=2] {'tc'}, dimensions={0}, use_global_device_ids=true | all-gather | bytes 98304 | tf_op jit(solution)/shard_map/all_gather | solution.py:63
  48.3 14.3 %all-gather.1 = bf16[4,1,4,1,64,64]{5,4,3,2,1,0:T(8,128)(2,1)S(1)} all-gather(bf16[1,1,4,1,64,64]{5,4,3,2,1,0:T(8,128)(2,1)S(1)} %fusion.68), channel_id=3, replica_groups=mesh['people'=2,'tz'=8,'ty'=4,'tc'=2,'type'=2] {'ty'}, dimensions={0}, use_global_device_ids=true | all-gather | bytes 163840 | tf_op jit(solution)/shard_map/all_gather | solution.py:63
  64.0 28.9 %all-gather.2 = bf16[8,1,4,1,64,64]{5,4,3,2,1,0:T(8,128)(2,1)S(1)} all-gather(bf16[1,1,4,1,64,64]{5,4,3,2,1,0:T(8,128)(2,1)S(1)} %fusion.69), channel_id=4, replica_groups=mesh['people'=2,'tz'=8,'ty'=4,'tc'=2,'type'=2] {'tz'}, dimensions={0}, use_global_device_ids=true | all-gather | bytes 294912 | tf_op jit(solution)/shard_map/all_gather | solution.py:63
  98.6 1.7 copy.317
  100.3 1.7 copy.316
  102.0 1.2 fusion.43
  106.3 2.7 %fusion.18 = (f32[4,16]{1,0:T(4,128)S(1)}, f32[4,16,64]{2,1,0:T(8,128)S(1)}) fusion(f32[4,1,32,64,64]{4,3,2,0,1:T(8,128)} %copy-done.4, f32[4,16,64]{2,1,0:T(8,128)S(1)} %bitcast.375), kind=kLoop, calls=%fused_computation.31 | loop fusion | flops 782272 | bytes 1081600 | tf_op jit(solution)/shard_map/reduce_sum | solution.py:32
  109.1 1.2 concatenate.46
  110.5 4.4 %fusion.13 = (f32[4,32]{1,0:T(4,128)S(1)}, f32[4,32,64]{2,1,0:T(8,128)S(1)}) fusion(f32[4,1,64,64,64]{4,3,2,0,1:T(8,128)} %copy-done.2, f32[4,32,64]{2,1,0:T(8,128)S(1)} %copy.284), kind=kLoop, calls=%fused_computation.23 | loop fusion | flops 1564544 | bytes 2163200 | tf_op jit(solution)/shard_map/reduce_sum | solution.py:32
  115.4 8.0 %multiply_reduce_fusion = (f32[4,64]{1,0:T(4,128)S(1)}, f32[4,64,64]{2,1,0:T(8,128)S(1)}) fusion(f32[4,64,64]{2,1,0:T(8,128)S(1)} %copy.288, f32[4,64]{1,0:T(4,128)S(1)} %get-tuple-element.81, f32[4,64,64,64]{3,2,1,0:T(8,128)} %copy-done.3, f32[4,64,64]{2,1,0:T(8,128)} %copy-done.9), kind=kLoop, calls=%fused_computation.6 | loop fusion | flops 5226240 | bytes 4392960 | tf_op jit(solution)/shard_map/reduce_sum | solution.py:32
  127.3 3.9 %psum.28 = f32[2,2,261]{0,2,1:T(8,128)S(1)} all-reduce(f32[2,2,261]{0,2,1:T(8,128)S(1)} %broadcast_multiply_fusion), channel_id=1, replica_groups=mesh['people'=2,'tz'=8,'ty'=4,'tc'=2,'type'=2] {'tc'}, use_global_device_ids=true, to_apply=%region_44.45 | all-reduce | flops 1044 | bytes 8352 | tf_op jit(solution)/shard_map/psum | solution.py:181
  131.2 20.9 %psum.29 = f32[2,2,261]{0,2,1:T(8,128)S(1)} all-reduce(f32[2,2,261]{0,2,1:T(8,128)S(1)} %psum.28), channel_id=1, replica_groups=mesh['people'=2,'tz'=8,'ty'=4,'tc'=2,'type'=2] {'ty'}, use_global_device_ids=true, to_apply=%region_45.46 | all-reduce | flops 1044 | bytes 8352 | tf_op jit(solution)/shard_map/psum | solution.py:181
  152.1 31.3 %psum.30 = f32[2,2,261]{0,2,1:T(8,128)S(1)} all-reduce(f32[2,2,261]{0,2,1:T(8,128)S(1)} %psum.29), channel_id=1, replica_groups=mesh['people'=2,'tz'=8,'ty'=4,'tc'=2,'type'=2] {'tz'}, use_global_device_ids=true, to_apply=%region_46.47 | all-reduce | flops 1044 | bytes 8352 | tf_op jit(solution)/shard_map/psum | solution.py:181
  183.5 18.1 %psum.31 = f32[2,2,261]{0,2,1:T(8,128)S(1)} all-reduce(f32[2,2,261]{0,2,1:T(8,128)S(1)} %psum.30), channel_id=1, replica_groups=mesh['people'=2,'tz'=8,'ty'=4,'tc'=2,'type'=2] {'people','type'}, use_global_device_ids=true, to_apply=%region_47.48 | all-reduce | flops 1044 | bytes 8352 | tf_op jit(solution)/shard_map/psum | solution.py:181
  (159 shorter events, 32.6 us)
Async XLA Ops:
  0.6 15.7 %copy-start = (bf16[3,128,128]{2,1,0:T(8,128)(2,1)S(1)}, bf16[3,128,128]{2,1,0:T(8,128)(2,1)}, u32[]{:S(2)}) copy-start(bf16[3,128,128]{2,1,0:T(8,128)(2,1)} %param.18) | copy-start | bytes 294916
  1.5 13.0 %collective-permute-start.1 = (bf16[3,1,5]{2,0,1:T(4,128)(2,1)S(1)}, bf16[3,1,5]{2,0,1:T(4,128)(2,1)S(1)}, u32[]{:S(2)}, u32[]{:S(2)}) collective-permute-start(bf16[3,1,5]{2,0,1:T(4,128)(2,1)S(1)} %get-tuple-element.76), channel_id=1, source_target_pairs={{2,0},{4,2},{6,4},{8,6},{10,8},{12,10},{14,12},{16,14},{18,16},{20... | collective-permute-start | bytes 98 | tf_op jit(solution)/shard_map/ppermute | solution.py:22
  2.7 11.7 %collective-permute-start = (bf16[3,1,5]{2,0,1:T(4,128)(2,1)S(1)}, bf16[3,1,5]{2,0,1:T(4,128)(2,1)S(1)}, u32[]{:S(2)}, u32[]{:S(2)}) collective-permute-start(bf16[3,1,5]{2,0,1:T(4,128)(2,1)S(1)} %get-tuple-element.75), channel_id=1, source_target_pairs={{0,2},{2,4},{4,6},{6,8},{8,10},{10,12},{12,14},{14,16},{16,18},{18... | collective-permute-start | bytes 98 | tf_op jit(solution)/shard_map/ppermute | solution.py:19
  19.9 9.6 %copy-start.9 = (f32[4,64,64]{2,1,0:T(8,128)}, f32[4,64,64]{2,1,0:T(8,128)S(1)}, u32[]{:S(2)}) copy-start(f32[4,64,64]{2,1,0:T(8,128)S(1)} %get-tuple-element.62) | copy-start | bytes 196612
  24.5 5.1 %copy-start.3 = (f32[4,64,64,64]{3,2,1,0:T(8,128)}, f32[4,64,64,64]{3,2,1,0:T(8,128)S(1)}, u32[]{:S(2)}) copy-start(f32[4,64,64,64]{3,2,1,0:T(8,128)S(1)} %get-tuple-element.82) | copy-start | bytes 12582916
  36.5 3.6 %copy-start.2 = (f32[4,1,64,64,64]{4,3,2,0,1:T(8,128)}, f32[4,1,64,64,64]{4,3,2,0,1:T(8,128)S(1)}, u32[]{:S(2)}) copy-start(f32[4,1,64,64,64]{4,3,2,0,1:T(8,128)S(1)} %divide_bitcast_fusion) | copy-start | bytes 12582916
  40.1 3.0 %copy-start.4 = (f32[4,1,32,64,64]{4,3,2,0,1:T(8,128)}, f32[4,1,32,64,64]{4,3,2,0,1:T(8,128)S(1)}, u32[]{:S(2)}) copy-start(f32[4,1,32,64,64]{4,3,2,0,1:T(8,128)S(1)} %divide_bitcast_fusion.1) | copy-start | bytes 6291460
  43.3 0.8 copy-start.5
  44.5 3.3 %copy-start.8 = (f32[4,1,2,64,64]{4,3,2,0,1:T(8,128)}, f32[4,1,2,64,64]{4,3,2,0,1:T(8,128)S(1)}, u32[]{:S(2)}) copy-start(f32[4,1,2,64,64]{4,3,2,0,1:T(8,128)S(1)} %divide_bitcast_fusion.9) | copy-start | bytes 393220
  105.3 9.6 %copy-start.6 = (f32[4,1,1,64]{2,3,0,1:T(8,128)S(1)}, f32[4,1,1,64]{2,3,0,1:T(8,128)}, u32[]{:S(2)}) copy-start(f32[4,1,1,64]{2,3,0,1:T(8,128)} %copy.290) | copy-start | bytes 3076
  105.3 9.7 %copy-start.7 = (f32[4,1,1,64]{2,3,0,1:T(8,128)S(1)}, f32[4,1,1,64]{2,3,0,1:T(8,128)}, u32[]{:S(2)}) copy-start(f32[4,1,1,64]{2,3,0,1:T(8,128)} %copy.291) | copy-start | bytes 3076
  110.3 13.5 %copy-start.11 = (f32[4,1,128,64]{2,3,0,1:T(8,128)S(1)}, f32[4,1,128,64]{2,3,0,1:T(8,128)}, u32[]{:S(2)}) copy-start(f32[4,1,128,64]{2,3,0,1:T(8,128)} %copy.316) | copy-start | bytes 393220
  110.4 13.8 %copy-start.10 = (f32[4,1,128,64]{2,3,0,1:T(8,128)S(1)}, f32[4,1,128,64]{2,3,0,1:T(8,128)}, u32[]{:S(2)}) copy-start(f32[4,1,128,64]{2,3,0,1:T(8,128)} %copy.317) | copy-start | bytes 393220
  115.3 89.0 %copy-start.1 = (bf16[3,128,128]{2,1,0:T(8,128)(2,1)S(1)}, bf16[3,128,128]{2,1,0:T(8,128)(2,1)}, u32[]{:S(2)}) copy-start(bf16[3,128,128]{2,1,0:T(8,128)(2,1)} %param.18) | copy-start | bytes 294916
  115.4 87.1 %copy-start.12 = (f32[8]{0:T(128)S(1)}, f32[8]{0:T(128)}, u32[]{:S(2)}) copy-start(f32[8]{0:T(128)} %param.23) | copy-start | bytes 100

commit v5 on v3

--- a/solution.py
+++ b/solution.py
@@ -175,10 +175,10 @@
         people_index * persons + jnp.arange(persons)[:, None] == jnp.arange(people_n)[None, :]
     ).astype(jnp.float32)
     half_hot = (type_index == jnp.arange(halves_n)).astype(jnp.float32)
+    for axis in TM[::-1]:
+        row = lax.psum(row, axis)
     table = person_hot[:, :, None, None] * half_hot[None, None, :, None] * row[:, None, None, :]
-    table = jnp.sum(table, axis=0)
-    for axis in TM[::-1] + (("people", "type"),):
-        table = lax.psum(table, axis)
+    table = lax.psum(jnp.sum(table, axis=0), ("people", "type"))
 
     full = table[:, :, :kinds].reshape(people_n, halves_n * kinds)
     rate_full = full / total_epochs

time: 200 us -> 174 us (0.87)
  blocking collectives: 120 us -> 93.1 us
    psum x4, blocking collectives: 74.2 us -> 47.2 us  [the longest x3 28.7 us: on_device(): row = lax.psum(row, axis)]
where the time goes in v5:
time: 174 us; the launch traced here: 172 us
  blocking collectives  93.1 us (54%)
  matrix products  33.4 us (19%)
  other arithmetic  25.9 us (15%)
  local copies, waits for them, and re-layouts  12.9 us (7%)
  starting transfers between devices  4.31 us (2%)
  between operations  2.79 us (2%)
    all_gather x3, blocking collectives, group_scan(): lax.all_gather(mats.astype(jnp.bfloat16), axis).astype(mats.dtype)  45.9 us
    psum x3, blocking collectives, on_device(): row = lax.psum(row, axis)  28.7 us
    psum x1, blocking collectives, on_device(): table = lax.psum(jnp.sum(table, axis=0), ('people', 'type'))  18.5 us
    dot_general x14, matrix products, mat_mat(): return jnp.einsum('...im,...ml->...il', a, b, precision=HIGH)  9.26 us
    unnamed x2, other arithmetic  8.83 us
    dot_general x5, matrix products, on_device(): jnp.einsum('kpni,kpnil->kpnl', entry, sibling, precision=HIGH)  5.62 us
    dot_general x1, matrix products, on_device(): jnp.einsum('kpjim,kml->kpjil', level, trans, precision=HIGH) * cols[3]  5.28 us
    dot_general x1, matrix products, on_device(): jnp.einsum('kpjim,kml->kpjil', pair, trans, precision=HIGH) * cols[1]  5.06 us
  transfers between devices with their start and end apart: 2, of which 0 were waited for; matrix products, arithmetic and copies ran while one was open for 4% of the time, Pallas kernels for 0%

profile of v5, /device:TPU:4, one launch (start us, length us, event | category | flops | bytes accessed | tf_op | source)
XLA Modules:
  0.0 172.4 jit_solution(5632532734432345015)
XLA Ops:
  1.5 1.3 collective-permute-start.1
  2.7 3.0 %collective-permute-start = (bf16[3,1,5]{2,0,1:T(4,128)(2,1)S(1)}, bf16[3,1,5]{2,0,1:T(4,128)(2,1)S(1)}, u32[]{:S(2)}, u32[]{:S(2)}) collective-permute-start(bf16[3,1,5]{2,0,1:T(4,128)(2,1)S(1)} %get-tuple-element.55), channel_id=1, source_target_pairs={{0,2},{2,4},{4,6},{6,8},{8,10},{10,12},{12,14},{14,16},{16,18},{18... | collective-permute-start | bytes 98 | tf_op jit(solution)/shard_map/ppermute | solution.py:19
  9.2 1.2 fusion.92
  16.4 1.3 bitcast_reduce_fusion
  19.9 4.6 %multiply_reduce_fusion.3 = (f32[4,64]{1,0:T(4,128)S(1)}, f32[4,64,64,64]{3,2,1,0:T(8,128)S(1)}) fusion(f32[4,64,64]{2,1,0:T(8,128)S(1)} %get-tuple-element.42, f32[4,64,64]{2,1,0:T(8,128)S(1)} %multiply_add_fusion, f32[4,64,64]{2,1,0:T(8,128)S(1)} %get-tuple-element.43), kind=kOutput, calls=%fused_computation.15 | convolution fusion | flops 405798656 | bytes 4391936 | tf_op jit(solution)/shard_map/kpjim,kml->kpjil/dot_general | solution.py:138
  24.5 5.1 %multiply_reduce_fusion.2 = (f32[4,64]{1,0:T(4,128)S(1)}, f32[4,64,64,64]{3,2,1,0:T(8,128)S(1)}) fusion(f32[4,64,64]{2,1,0:T(8,128)S(1)} %get-tuple-element.41, f32[4,64,64]{2,1,0:T(8,128)S(1)} %multiply_add_fusion, f32[4,64,64,64]{3,2,1,0:T(8,128)S(1)} %get-tuple-element.62, f32[4,64]{1,0:T(4,128)S(1)} %get-tuple-element.61, ...), kind=kOutput, calls=%fused_computation.13 | convolution fusion | flops 406847232 | bytes 8587264 | tf_op jit(solution)/shard_map/kpjim,kml->kpjil/dot_general | solution.py:139
  29.6 5.3 %multiply_reduce_fusion.1 = (f32[4,64]{1,0:T(4,128)S(1)}, f32[4,64,64,64]{3,2,1,0:T(8,128)S(1)}) fusion(f32[4,64,64]{2,1,0:T(8,128)S(1)} %get-tuple-element.40, f32[4,64,64]{2,1,0:T(8,128)S(1)} %multiply_add_fusion, f32[4,64,64,64]{3,2,1,0:T(8,128)S(1)} %get-tuple-element.64, f32[4,64]{1,0:T(4,128)S(1)} %get-tuple-element.63, ...), kind=kOutput, calls=%fused_computation.11 | convolution fusion | flops 406847232 | bytes 8587264 | tf_op jit(solution)/shard_map/kpjim,kml->kpjil/dot_general | solution.py:140
  34.8 1.7 divide_bitcast_fusion
  36.5 3.1 %fusion.93 = (f32[4,32]{1,0:T(4,128)S(1)}, f32[4,32,64,64]{3,2,1,0:T(8,128)S(1)}) fusion(f32[4,1,64,64,64]{4,3,2,0,1:T(8,128)S(1)} %divide_bitcast_fusion), kind=kOutput, calls=%fused_computation.217 | convolution fusion | flops 201850752 | bytes 6291968 | tf_op jit(solution)/shard_map/...im,...ml->...il/dot_general | solution.py:36
  40.1 1.4 fusion.94
  44.9 2.7 %all-gather = bf16[8,64,64]{2,1,0:T(8,128)(2,1)S(1)} all-gather(bf16[4,64,64]{2,1,0:T(8,128)(2,1)S(1)} %divide_convert_fusion), channel_id=2, replica_groups=mesh['people'=2,'tz'=8,'ty'=4,'tc'=2,'type'=2] {'tc'}, dimensions={0}, use_global_device_ids=true | all-gather | bytes 98304 | tf_op jit(solution)/shard_map/all_gather | solution.py:63
  48.3 14.3 %all-gather.1 = bf16[4,1,4,1,64,64]{5,4,3,2,1,0:T(8,128)(2,1)S(1)} all-gather(bf16[1,1,4,1,64,64]{5,4,3,2,1,0:T(8,128)(2,1)S(1)} %fusion.64), channel_id=3, replica_groups=mesh['people'=2,'tz'=8,'ty'=4,'tc'=2,'type'=2] {'ty'}, dimensions={0}, use_global_device_ids=true | all-gather | bytes 163840 | tf_op jit(solution)/shard_map/all_gather | solution.py:63
  64.0 28.9 %all-gather.2 = bf16[8,1,4,1,64,64]{5,4,3,2,1,0:T(8,128)(2,1)S(1)} all-gather(bf16[1,1,4,1,64,64]{5,4,3,2,1,0:T(8,128)(2,1)S(1)} %fusion.65), channel_id=4, replica_groups=mesh['people'=2,'tz'=8,'ty'=4,'tc'=2,'type'=2] {'tz'}, dimensions={0}, use_global_device_ids=true | all-gather | bytes 294912 | tf_op jit(solution)/shard_map/all_gather | solution.py:63
  95.9 1.1 fusion.63
  98.1 1.2 fusion.41
  100.0 1.6 fusion.26
  104.2 2.5 %fusion.17 = f32[4,16,1,64]{3,2,1,0:T(1,128)S(1)} fusion(f32[4,16,64,1]{2,3,1,0:T(1,128)S(1)} %bitcast.433, f32[4,1,32,64,64]{4,3,2,0,1:T(8,128)} %copy-done.4), kind=kOutput, calls=%fused_computation.30 | convolution fusion | flops 1572864 | bytes 2129920 | tf_op jit(solution)/shard_map/kpni,kpnil->kpnl/dot_general | solution.py:155
  107.0 1.3 concatenate.46
  108.4 2.9 %multiply_reduce_fusion.4 = f32[4,32,64]{2,1,0:T(8,128)S(1)} fusion(f32[4,1,64,64,64]{4,3,2,0,1:T(8,128)} %copy-done.2, f32[4,32,64]{2,1,0:T(8,128)S(1)} %copy.260), kind=kLoop, calls=%fused_computation.19 | loop fusion | flops 1040384 | bytes 2162688
  112.0 5.9 %multiply_reduce_fusion = f32[4,64,64]{2,1,0:T(8,128)S(1)} fusion(f32[4,64,64]{2,1,0:T(8,128)S(1)} %copy.261, f32[4,64]{1,0:T(4,128)S(1)} %get-tuple-element.61, f32[4,64,64,64]{3,2,1,0:T(8,128)} %copy-done.3, f32[4,64,64]{2,1,0:T(8,128)} %copy-done.9), kind=kLoop, calls=%fused_computation.5 | loop fusion | flops 4177920 | bytes 4391936
  121.3 2.4 %psum.28 = f32[1,261]{1,0:T(1,128)S(1)} all-reduce(f32[1,261]{1,0:T(1,128)S(1)} %pad_maximum_fusion.5), channel_id=1, replica_groups=mesh['people'=2,'tz'=8,'ty'=4,'tc'=2,'type'=2] {'tc'}, use_global_device_ids=true, to_apply=%region_36.37 | all-reduce | flops 261 | bytes 2088 | tf_op jit(solution)/shard_map/psum | solution.py:179
  123.7 11.0 %psum.29 = f32[1,261]{1,0:T(1,128)S(1)} all-reduce(f32[1,261]{1,0:T(1,128)S(1)} %psum.28), channel_id=1, replica_groups=mesh['people'=2,'tz'=8,'ty'=4,'tc'=2,'type'=2] {'ty'}, use_global_device_ids=true, to_apply=%region_37.38 | all-reduce | flops 261 | bytes 2088 | tf_op jit(solution)/shard_map/psum | solution.py:179
  134.8 15.2 %psum.30 = f32[261]{0:T(512)S(1)} all-reduce(f32[261]{0:T(512)S(1)} %reduce.64), channel_id=1, replica_groups=mesh['people'=2,'tz'=8,'ty'=4,'tc'=2,'type'=2] {'tz'}, use_global_device_ids=true, to_apply=%region_38.39 | all-reduce | flops 261 | bytes 2088 | tf_op jit(solution)/shard_map/psum | solution.py:179
  150.1 18.5 %psum.31 = f32[2,2,261]{0,2,1:T(8,128)S(1)} all-reduce(f32[2,2,261]{0,2,1:T(8,128)S(1)} %broadcast_multiply_fusion), channel_id=1, replica_groups=mesh['people'=2,'tz'=8,'ty'=4,'tc'=2,'type'=2] {'people','type'}, use_global_device_ids=true, to_apply=%region_39.40 | all-reduce | flops 1044 | bytes 8352 | tf_op jit(solution)/shard_map/psum | solution.py:181
  (162 shorter events, 32.2 us)
Async XLA Ops:
  0.6 15.7 %copy-start = (bf16[3,128,128]{2,1,0:T(8,128)(2,1)S(1)}, bf16[3,128,128]{2,1,0:T(8,128)(2,1)}, u32[]{:S(2)}) copy-start(bf16[3,128,128]{2,1,0:T(8,128)(2,1)} %param.18) | copy-start | bytes 294916
  1.5 13.0 %collective-permute-start.1 = (bf16[3,1,5]{2,0,1:T(4,128)(2,1)S(1)}, bf16[3,1,5]{2,0,1:T(4,128)(2,1)S(1)}, u32[]{:S(2)}, u32[]{:S(2)}) collective-permute-start(bf16[3,1,5]{2,0,1:T(4,128)(2,1)S(1)} %get-tuple-element.56), channel_id=1, source_target_pairs={{2,0},{4,2},{6,4},{8,6},{10,8},{12,10},{14,12},{16,14},{18,16},{20... | collective-permute-start | bytes 98 | tf_op jit(solution)/shard_map/ppermute | solution.py:22
  2.7 11.7 %collective-permute-start = (bf16[3,1,5]{2,0,1:T(4,128)(2,1)S(1)}, bf16[3,1,5]{2,0,1:T(4,128)(2,1)S(1)}, u32[]{:S(2)}, u32[]{:S(2)}) collective-permute-start(bf16[3,1,5]{2,0,1:T(4,128)(2,1)S(1)} %get-tuple-element.55), channel_id=1, source_target_pairs={{0,2},{2,4},{4,6},{6,8},{8,10},{10,12},{12,14},{14,16},{16,18},{18... | collective-permute-start | bytes 98 | tf_op jit(solution)/shard_map/ppermute | solution.py:19
  19.9 9.6 %copy-start.9 = (f32[4,64,64]{2,1,0:T(8,128)}, f32[4,64,64]{2,1,0:T(8,128)S(1)}, u32[]{:S(2)}) copy-start(f32[4,64,64]{2,1,0:T(8,128)S(1)} %get-tuple-element.42) | copy-start | bytes 196612
  24.5 5.1 %copy-start.3 = (f32[4,64,64,64]{3,2,1,0:T(8,128)}, f32[4,64,64,64]{3,2,1,0:T(8,128)S(1)}, u32[]{:S(2)}) copy-start(f32[4,64,64,64]{3,2,1,0:T(8,128)S(1)} %get-tuple-element.62) | copy-start | bytes 12582916
  36.5 3.6 %copy-start.2 = (f32[4,1,64,64,64]{4,3,2,0,1:T(8,128)}, f32[4,1,64,64,64]{4,3,2,0,1:T(8,128)S(1)}, u32[]{:S(2)}) copy-start(f32[4,1,64,64,64]{4,3,2,0,1:T(8,128)S(1)} %divide_bitcast_fusion) | copy-start | bytes 12582916
  40.1 3.0 %copy-start.4 = (f32[4,1,32,64,64]{4,3,2,0,1:T(8,128)}, f32[4,1,32,64,64]{4,3,2,0,1:T(8,128)S(1)}, u32[]{:S(2)}) copy-start(f32[4,1,32,64,64]{4,3,2,0,1:T(8,128)S(1)} %divide_bitcast_fusion.1) | copy-start | bytes 6291460
  43.3 0.8 copy-start.5
  44.5 3.3 %copy-start.8 = (f32[4,1,2,64,64]{4,3,2,0,1:T(8,128)}, f32[4,1,2,64,64]{4,3,2,0,1:T(8,128)S(1)}, u32[]{:S(2)}) copy-start(f32[4,1,2,64,64]{4,3,2,0,1:T(8,128)S(1)} %divide_bitcast_fusion.9) | copy-start | bytes 393220
  103.0 8.6 %copy-start.6 = (f32[4,1,1,64]{2,3,0,1:T(8,128)S(1)}, f32[4,1,1,64]{2,3,0,1:T(8,128)}, u32[]{:S(2)}) copy-start(f32[4,1,1,64]{2,3,0,1:T(8,128)} %copy.208) | copy-start | bytes 3076
  103.0 8.6 %copy-start.7 = (f32[4,1,2,64]{2,3,0,1:T(8,128)S(1)}, f32[4,1,2,64]{2,3,0,1:T(8,128)}, u32[]{:S(2)}) copy-start(f32[4,1,2,64]{2,3,0,1:T(8,128)} %fusion.26) | copy-start | bytes 6148
  106.9 11.2 %copy-start.11 = (f32[4,1,128,64]{3,2,0,1:T(8,128)S(1)}, f32[4,1,128,64]{3,2,0,1:T(8,128)}, u32[]{:S(2)}) copy-start(f32[4,1,128,64]{3,2,0,1:T(8,128)} %get-tuple-element.45) | copy-start | bytes 393220
  107.0 11.2 %copy-start.10 = (f32[4,1,128,64]{3,2,0,1:T(8,128)S(1)}, f32[4,1,128,64]{3,2,0,1:T(8,128)}, u32[]{:S(2)}) copy-start(f32[4,1,128,64]{3,2,0,1:T(8,128)} %get-tuple-element.44) | copy-start | bytes 393220
  111.8 60.5 %copy-start.1 = (bf16[3,128,128]{2,1,0:T(8,128)(2,1)S(1)}, bf16[3,128,128]{2,1,0:T(8,128)(2,1)}, u32[]{:S(2)}) copy-start(bf16[3,128,128]{2,1,0:T(8,128)(2,1)} %param.18) | copy-start | bytes 294916
  111.9 57.0 %copy-start.12 = (f32[8]{0:T(128)S(1)}, f32[8]{0:T(128)}, u32[]{:S(2)}) copy-start(f32[8]{0:T(128)} %param.23) | copy-start | bytes 100

commit v6 on v5

--- a/solution.py
+++ b/solution.py
@@ -177,8 +177,10 @@
     half_hot = (type_index == jnp.arange(halves_n)).astype(jnp.float32)
     for axis in TM[::-1]:
         row = lax.psum(row, axis)
-    table = person_hot[:, :, None, None] * half_hot[None, None, :, None] * row[:, None, None, :]
-    table = lax.psum(jnp.sum(table, axis=0), ("people", "type"))
+    gathered = lax.all_gather(row, ("people", "type"))
+    table = jnp.transpose(
+        gathered.reshape((people_n // persons, halves_n) + row.shape), (0, 2, 1, 3)
+    ).reshape(people_n, halves_n, row.shape[-1])
 
     full = table[:, :, :kinds].reshape(people_n, halves_n * kinds)
     rate_full = full / total_epochs

time: 174 us -> 166 us (0.954)
  blocking collectives: 93.1 us -> 84.7 us
    psum x1 -> x0, blocking collectives: 18.5 us -> none  [on_device(): table = lax.psum(jnp.sum(table, axis=0), ('people', 'type'))]
    all_gather x0 -> x1, blocking collectives: none -> 10.1 us  [on_device(): gathered = lax.all_gather(row, ('people', 'type'))]
where the time goes in v6:
time: 166 us; the launch traced here: 164 us
  blocking collectives  84.7 us (51%)
  matrix products  33.3 us (20%)
  other arithmetic  25.8 us (16%)
  local copies, waits for them, and re-layouts  13.2 us (8%)
  starting transfers between devices  4.31 us (3%)
  between operations  2.76 us (2%)
    all_gather x3, blocking collectives, group_scan(): lax.all_gather(mats.astype(jnp.bfloat16), axis).astype(mats.dtype)  45.9 us
    psum x3, blocking collectives, on_device(): row = lax.psum(row, axis)  28.7 us
    all_gather x1, blocking collectives, on_device(): gathered = lax.all_gather(row, ('people', 'type'))  10.1 us
    dot_general x14, matrix products, mat_mat(): return jnp.einsum('...im,...ml->...il', a, b, precision=HIGH)  9.27 us
    unnamed x2, other arithmetic  8.83 us
    dot_general x5, matrix products, on_device(): jnp.einsum('kpni,kpnil->kpnl', entry, sibling, precision=HIGH)  5.62 us
    dot_general x1, matrix products, on_device(): jnp.einsum('kpjim,kml->kpjil', level, trans, precision=HIGH) * cols[3]  5.28 us
    dot_general x1, matrix products, on_device(): jnp.einsum('kpjim,kml->kpjil', pair, trans, precision=HIGH) * cols[1]  5.06 us
  transfers between devices with their start and end apart: 2, of which 0 were waited for; matrix products, arithmetic and copies ran while one was open for 4% of the time, Pallas kernels for 0%

profile of v6, /device:TPU:4, one launch (start us, length us, event | category | flops | bytes accessed | tf_op | source)
XLA Modules:
  0.0 164.2 jit_solution(14035067492311760216)
XLA Ops:
  1.5 1.3 collective-permute-start.1
  2.7 3.0 %collective-permute-start = (bf16[3,1,5]{2,0,1:T(4,128)(2,1)S(1)}, bf16[3,1,5]{2,0,1:T(4,128)(2,1)S(1)}, u32[]{:S(2)}, u32[]{:S(2)}) collective-permute-start(bf16[3,1,5]{2,0,1:T(4,128)(2,1)S(1)} %get-tuple-element.55), channel_id=1, source_target_pairs={{0,2},{2,4},{4,6},{6,8},{8,10},{10,12},{12,14},{14,16},{16,18},{18... | collective-permute-start | bytes 98 | tf_op jit(solution)/shard_map/ppermute | solution.py:19
  9.2 1.2 fusion.94
  16.3 1.3 bitcast_reduce_fusion
  19.8 4.6 %multiply_reduce_fusion.3 = (f32[4,64]{1,0:T(4,128)S(1)}, f32[4,64,64,64]{3,2,1,0:T(8,128)S(1)}) fusion(f32[4,64,64]{2,1,0:T(8,128)S(1)} %get-tuple-element.42, f32[4,64,64]{2,1,0:T(8,128)S(1)} %multiply_add_fusion, f32[4,64,64]{2,1,0:T(8,128)S(1)} %get-tuple-element.43), kind=kOutput, calls=%fused_computation.15 | convolution fusion | flops 405798656 | bytes 4391936 | tf_op jit(solution)/shard_map/kpjim,kml->kpjil/dot_general | solution.py:138
  24.4 5.1 %multiply_reduce_fusion.2 = (f32[4,64]{1,0:T(4,128)S(1)}, f32[4,64,64,64]{3,2,1,0:T(8,128)S(1)}) fusion(f32[4,64,64]{2,1,0:T(8,128)S(1)} %get-tuple-element.41, f32[4,64,64]{2,1,0:T(8,128)S(1)} %multiply_add_fusion, f32[4,64,64,64]{3,2,1,0:T(8,128)S(1)} %get-tuple-element.62, f32[4,64]{1,0:T(4,128)S(1)} %get-tuple-element.61, ...), kind=kOutput, calls=%fused_computation.13 | convolution fusion | flops 406847232 | bytes 8587264 | tf_op jit(solution)/shard_map/kpjim,kml->kpjil/dot_general | solution.py:139
  29.5 5.3 %multiply_reduce_fusion.1 = (f32[4,64]{1,0:T(4,128)S(1)}, f32[4,64,64,64]{3,2,1,0:T(8,128)S(1)}) fusion(f32[4,64,64]{2,1,0:T(8,128)S(1)} %get-tuple-element.40, f32[4,64,64]{2,1,0:T(8,128)S(1)} %multiply_add_fusion, f32[4,64,64,64]{3,2,1,0:T(8,128)S(1)} %get-tuple-element.64, f32[4,64]{1,0:T(4,128)S(1)} %get-tuple-element.63, ...), kind=kOutput, calls=%fused_computation.11 | convolution fusion | flops 406847232 | bytes 8587264 | tf_op jit(solution)/shard_map/kpjim,kml->kpjil/dot_general | solution.py:140
  34.8 1.7 %divide_bitcast_fusion = f32[4,1,64,64,64]{4,3,2,0,1:T(8,128)S(1)} fusion(f32[4,64,64,64]{3,2,1,0:T(8,128)S(1)} %get-tuple-element.66, f32[4,64]{1,0:T(4,128)S(1)} %get-tuple-element.65, f32[4,64,64]{2,1,0:T(8,128)S(1)} %get-tuple-element.40), kind=kLoop, calls=%fused_computation.6 | loop fusion | flops 2097152 | bytes 8455168 | tf_op jit(solution)/shard_map/div | solution.py:28
  36.4 3.1 %fusion.95 = (f32[4,32]{1,0:T(4,128)S(1)}, f32[4,32,64,64]{3,2,1,0:T(8,128)S(1)}) fusion(f32[4,1,64,64,64]{4,3,2,0,1:T(8,128)S(1)} %divide_bitcast_fusion), kind=kOutput, calls=%fused_computation.217 | convolution fusion | flops 201850752 | bytes 6291968 | tf_op jit(solution)/shard_map/...im,...ml->...il/dot_general | solution.py:36
  40.0 1.4 fusion.96
  44.8 2.7 %all-gather = bf16[8,64,64]{2,1,0:T(8,128)(2,1)S(1)} all-gather(bf16[4,64,64]{2,1,0:T(8,128)(2,1)S(1)} %divide_convert_fusion), channel_id=2, replica_groups=mesh['people'=2,'tz'=8,'ty'=4,'tc'=2,'type'=2] {'tc'}, dimensions={0}, use_global_device_ids=true | all-gather | bytes 98304 | tf_op jit(solution)/shard_map/all_gather | solution.py:63
  48.3 14.3 %all-gather.1 = bf16[4,1,4,1,64,64]{5,4,3,2,1,0:T(8,128)(2,1)S(1)} all-gather(bf16[1,1,4,1,64,64]{5,4,3,2,1,0:T(8,128)(2,1)S(1)} %fusion.64), channel_id=3, replica_groups=mesh['people'=2,'tz'=8,'ty'=4,'tc'=2,'type'=2] {'ty'}, dimensions={0}, use_global_device_ids=true | all-gather | bytes 163840 | tf_op jit(solution)/shard_map/all_gather | solution.py:63
  63.9 28.9 %all-gather.2 = bf16[8,1,4,1,64,64]{5,4,3,2,1,0:T(8,128)(2,1)S(1)} all-gather(bf16[1,1,4,1,64,64]{5,4,3,2,1,0:T(8,128)(2,1)S(1)} %fusion.65), channel_id=4, replica_groups=mesh['people'=2,'tz'=8,'ty'=4,'tc'=2,'type'=2] {'tz'}, dimensions={0}, use_global_device_ids=true | all-gather | bytes 294912 | tf_op jit(solution)/shard_map/all_gather | solution.py:63
  95.9 1.1 fusion.63
  98.0 1.2 fusion.41
  99.9 1.6 fusion.26
  104.2 2.5 %fusion.17 = f32[4,16,1,64]{3,2,1,0:T(1,128)S(1)} fusion(f32[4,16,64,1]{2,3,1,0:T(1,128)S(1)} %bitcast.432, f32[4,1,32,64,64]{4,3,2,0,1:T(8,128)} %copy-done.4), kind=kOutput, calls=%fused_computation.30 | convolution fusion | flops 1572864 | bytes 2129920 | tf_op jit(solution)/shard_map/kpni,kpnil->kpnl/dot_general | solution.py:155
  106.9 1.3 concatenate.46
  108.3 2.9 %multiply_reduce_fusion.4 = f32[4,32,64]{2,1,0:T(8,128)S(1)} fusion(f32[4,1,64,64,64]{4,3,2,0,1:T(8,128)} %copy-done.2, f32[4,32,64]{2,1,0:T(8,128)S(1)} %copy.250), kind=kLoop, calls=%fused_computation.19 | loop fusion | flops 1040384 | bytes 2162688
  111.9 5.9 %multiply_reduce_fusion = f32[4,64,64]{2,1,0:T(8,128)S(1)} fusion(f32[4,64,64]{2,1,0:T(8,128)S(1)} %copy.251, f32[4,64]{1,0:T(4,128)S(1)} %get-tuple-element.61, f32[4,64,64,64]{3,2,1,0:T(8,128)} %copy-done.3, f32[4,64,64]{2,1,0:T(8,128)} %copy-done.9), kind=kLoop, calls=%fused_computation.5 | loop fusion | flops 4177920 | bytes 4391936
  121.2 2.4 %psum.21 = f32[1,261]{1,0:T(1,128)S(1)} all-reduce(f32[1,261]{1,0:T(1,128)S(1)} %pad_maximum_fusion.5), channel_id=1, replica_groups=mesh['people'=2,'tz'=8,'ty'=4,'tc'=2,'type'=2] {'tc'}, use_global_device_ids=true, to_apply=%region_36.37 | all-reduce | flops 261 | bytes 2088 | tf_op jit(solution)/shard_map/psum | solution.py:179
  123.6 11.0 %psum.22 = f32[1,261]{1,0:T(1,128)S(1)} all-reduce(f32[1,261]{1,0:T(1,128)S(1)} %psum.21), channel_id=1, replica_groups=mesh['people'=2,'tz'=8,'ty'=4,'tc'=2,'type'=2] {'ty'}, use_global_device_ids=true, to_apply=%region_37.38 | all-reduce | flops 261 | bytes 2088 | tf_op jit(solution)/shard_map/psum | solution.py:179
  134.7 15.2 %psum.23 = f32[1,1,261]{2,1,0:T(1,128)S(1)} all-reduce(f32[1,1,261]{2,1,0:T(1,128)S(1)} %bitcast.450), channel_id=1, replica_groups=mesh['people'=2,'tz'=8,'ty'=4,'tc'=2,'type'=2] {'tz'}, use_global_device_ids=true, to_apply=%region_38.39 | all-reduce | flops 261 | bytes 2088 | tf_op jit(solution)/shard_map/psum | solution.py:179
  149.9 10.1 %all_gather.22 = f32[4,1,261]{2,1,0:T(1,128)S(1)} all-gather(f32[1,1,261]{2,1,0:T(1,128)S(1)} %psum.23), channel_id=1, replica_groups=mesh['people'=2,'tz'=8,'ty'=4,'tc'=2,'type'=2] {'people','type'}, dimensions={0}, use_global_device_ids=true | all-gather | bytes 5220 | tf_op jit(solution)/shard_map/all_gather | solution.py:180
  (163 shorter events, 32.4 us)
Async XLA Ops:
  0.6 15.6 %copy-start = (bf16[3,128,128]{2,1,0:T(8,128)(2,1)S(1)}, bf16[3,128,128]{2,1,0:T(8,128)(2,1)}, u32[]{:S(2)}) copy-start(bf16[3,128,128]{2,1,0:T(8,128)(2,1)} %param.18) | copy-start | bytes 294916
  1.5 12.9 %collective-permute-start.1 = (bf16[3,1,5]{2,0,1:T(4,128)(2,1)S(1)}, bf16[3,1,5]{2,0,1:T(4,128)(2,1)S(1)}, u32[]{:S(2)}, u32[]{:S(2)}) collective-permute-start(bf16[3,1,5]{2,0,1:T(4,128)(2,1)S(1)} %get-tuple-element.56), channel_id=1, source_target_pairs={{2,0},{4,2},{6,4},{8,6},{10,8},{12,10},{14,12},{16,14},{18,16},{20... | collective-permute-start | bytes 98 | tf_op jit(solution)/shard_map/ppermute | solution.py:22
  2.7 11.6 %collective-permute-start = (bf16[3,1,5]{2,0,1:T(4,128)(2,1)S(1)}, bf16[3,1,5]{2,0,1:T(4,128)(2,1)S(1)}, u32[]{:S(2)}, u32[]{:S(2)}) collective-permute-start(bf16[3,1,5]{2,0,1:T(4,128)(2,1)S(1)} %get-tuple-element.55), channel_id=1, source_target_pairs={{0,2},{2,4},{4,6},{6,8},{8,10},{10,12},{12,14},{14,16},{16,18},{18... | collective-permute-start | bytes 98 | tf_op jit(solution)/shard_map/ppermute | solution.py:19
  19.8 9.6 %copy-start.9 = (f32[4,64,64]{2,1,0:T(8,128)}, f32[4,64,64]{2,1,0:T(8,128)S(1)}, u32[]{:S(2)}) copy-start(f32[4,64,64]{2,1,0:T(8,128)S(1)} %get-tuple-element.42) | copy-start | bytes 196612
  24.4 5.1 %copy-start.3 = (f32[4,64,64,64]{3,2,1,0:T(8,128)}, f32[4,64,64,64]{3,2,1,0:T(8,128)S(1)}, u32[]{:S(2)}) copy-start(f32[4,64,64,64]{3,2,1,0:T(8,128)S(1)} %get-tuple-element.62) | copy-start | bytes 12582916
  36.4 3.6 %copy-start.2 = (f32[4,1,64,64,64]{4,3,2,0,1:T(8,128)}, f32[4,1,64,64,64]{4,3,2,0,1:T(8,128)S(1)}, u32[]{:S(2)}) copy-start(f32[4,1,64,64,64]{4,3,2,0,1:T(8,128)S(1)} %divide_bitcast_fusion) | copy-start | bytes 12582916
  40.0 3.0 %copy-start.4 = (f32[4,1,32,64,64]{4,3,2,0,1:T(8,128)}, f32[4,1,32,64,64]{4,3,2,0,1:T(8,128)S(1)}, u32[]{:S(2)}) copy-start(f32[4,1,32,64,64]{4,3,2,0,1:T(8,128)S(1)} %divide_bitcast_fusion.1) | copy-start | bytes 6291460
  43.2 0.8 copy-start.5
  44.4 3.3 %copy-start.8 = (f32[4,1,2,64,64]{4,3,2,0,1:T(8,128)}, f32[4,1,2,64,64]{4,3,2,0,1:T(8,128)S(1)}, u32[]{:S(2)}) copy-start(f32[4,1,2,64,64]{4,3,2,0,1:T(8,128)S(1)} %divide_bitcast_fusion.9) | copy-start | bytes 393220
  102.9 8.6 %copy-start.6 = (f32[4,1,1,64]{2,3,0,1:T(8,128)S(1)}, f32[4,1,1,64]{2,3,0,1:T(8,128)}, u32[]{:S(2)}) copy-start(f32[4,1,1,64]{2,3,0,1:T(8,128)} %copy.200) | copy-start | bytes 3076
  102.9 8.6 %copy-start.7 = (f32[4,1,2,64]{2,3,0,1:T(8,128)S(1)}, f32[4,1,2,64]{2,3,0,1:T(8,128)}, u32[]{:S(2)}) copy-start(f32[4,1,2,64]{2,3,0,1:T(8,128)} %fusion.26) | copy-start | bytes 6148
  106.8 11.2 %copy-start.11 = (f32[4,1,128,64]{3,2,0,1:T(8,128)S(1)}, f32[4,1,128,64]{3,2,0,1:T(8,128)}, u32[]{:S(2)}) copy-start(f32[4,1,128,64]{3,2,0,1:T(8,128)} %get-tuple-element.45) | copy-start | bytes 393220
  106.9 11.2 %copy-start.10 = (f32[4,1,128,64]{3,2,0,1:T(8,128)S(1)}, f32[4,1,128,64]{3,2,0,1:T(8,128)}, u32[]{:S(2)}) copy-start(f32[4,1,128,64]{3,2,0,1:T(8,128)} %get-tuple-element.44) | copy-start | bytes 393220
  111.7 49.0 %copy-start.12 = (f32[8]{0:T(128)S(1)}, f32[8]{0:T(128)}, u32[]{:S(2)}) copy-start(f32[8]{0:T(128)} %param.23) | copy-start | bytes 100
  111.8 52.4 %copy-start.1 = (bf16[3,128,128]{2,1,0:T(8,128)(2,1)S(1)}, bf16[3,128,128]{2,1,0:T(8,128)(2,1)}, u32[]{:S(2)}) copy-start(bf16[3,128,128]{2,1,0:T(8,128)(2,1)} %param.18) | copy-start | bytes 294916
